TPU v7x, 512 devices: a whole 4x8x8 slice. The times are simulated.
512 devices in a mesh: tau: 8 (over x, core), blk: 64 (over z, y).
Axes of the slice: x: 4, y: 8, z: 8, core: 2. Of those that a mesh axis runs over, the one named last changes fastest.
Arguments:
- three_center: bfloat16 [64, 128, 128, 128], P('blk'), may hold values from -0.59765625 to 0.59765625
- green_blocks: bfloat16 [8, 512, 2048], P('tau', 'blk'), may hold values from -0.5 to 0.5
- block_owner: int32 [3072], P('blk'), may hold values from 0 to 63, as said below
- block_slot: int32 [3072], P('blk'), may hold values from 0 to 7
- fold_weights: float32 [8, 8], P(None, 'tau'), may hold values from -1 to 1
Outputs:
- chi_freq: float32 [8, 8192, 384], P('tau', 'blk')
Inputs may be any that keep to these rules, and one draw needn't show every extreme that they name: `block_owner`: among the 48 entries of each auxiliary block, no owner appears more than 2 times, and one owner appears exactly 2 times in the entries of every auxiliary block.
All inputs are finite; a program needn't handle non-finite values.
Results may differ from a plain program's by a relative error of at most 0.0041.
Values may be sent and summed in bfloat16 or wider, within the bound.
No kernel may reach another device: no remote copies, remote signals or barrier semaphores. Data moves between devices by JAX's collectives and lax.ppermute only.
A program may use at most 128 MiB of HBM per device.

v0:
```python
import jax
import jax.numpy as jnp
from jax import lax
from jax.sharding import PartitionSpec as P


AB = 32
NS = 4
HALF = 1


def from_behind(value, axis, by):
    size = lax.axis_size(axis)
    return lax.ppermute(value, axis, [(i, (i + by) % size) for i in range(size)])


def green_pair(blocks):
    blocks = blocks.reshape(NS, NS, 2, AB, AB)
    occupied = blocks[:, :, 0].transpose(0, 2, 1, 3).reshape(NS * AB, NS * AB)
    virtual = blocks[:, :, 1].transpose(0, 2, 1, 3).reshape(NS * AB, NS * AB)
    return (occupied, virtual)


def image_of(occupied, virtual, source_t):
    halfway = lax.dot_general(
        source_t, virtual, (((2,), (1,)), ((), ())), preferred_element_type=jnp.float32
    ).astype(jnp.bfloat16)
    image = lax.dot_general(
        halfway, occupied, (((1,), (1,)), ((), ())), preferred_element_type=jnp.float32
    ).astype(jnp.bfloat16)
    return image


def pair_block(partner_t, image):
    aux_width = image.shape[0]
    flat_image = image.reshape(aux_width, -1)
    flat_partner = partner_t.reshape(flat_image.shape[1], -1)
    return jnp.dot(flat_image, flat_partner, preferred_element_type=jnp.float32)


def split_pair_block(halves, image):
    core = lax.axis_index("tau") % 2
    half = image.shape[1] // 2
    mine = lax.dynamic_slice_in_dim(image, core * half, half, 1)
    theirs = lax.dynamic_slice_in_dim(image, (1 - core) * half, half, 1)
    return pair_block(halves[0], mine) + pair_block(halves[1], theirs)


def partner_from(own_t, by, chunks=2):
    core = lax.axis_index("tau") % 2
    half = own_t.shape[0] // 2
    step = half // chunks
    size = lax.axis_size("tau")
    fetched, other = [], []
    for k in range(chunks):
        mine = lax.dynamic_slice_in_dim(own_t, core * half + k * step, step, 0)
        got = from_behind(mine, "blk", by)
        fetched.append(got)
        other.append(lax.ppermute(got, "tau", [(i, i ^ 1) for i in range(size)]))
    return jnp.concatenate(fetched, axis=0), jnp.concatenate(other, axis=0)


def local_body(three_center, green_blocks, block_owner, block_slot, fold_weights):
    source = three_center[0]
    source_t = jnp.transpose(source, (2, 0, 1))
    own_t = jnp.transpose(source, (1, 0, 2))
    partners = [partner_from(own_t, HALF - j) if j != HALF else own_t for j in range(2 * HALF + 1)]
    local_table = green_blocks[0]
    devices = lax.axis_size("blk")
    requests = block_owner.shape[0]
    per_slot = NS * NS
    capacity = 2 * ((requests + devices - 1) // devices)
    owner_match = (block_owner[:, None] == jnp.arange(devices, dtype=jnp.int32)[None, :]).astype(
        jnp.int32
    )
    position = jnp.sum(jnp.cumsum(owner_match, axis=0) * owner_match, axis=1) - 1
    outgoing = jnp.zeros((devices, capacity), jnp.int32).at[block_owner, position].set(block_slot)
    asked = lax.all_to_all(outgoing, "blk", split_axis=0, concat_axis=0, tiled=True)
    found_blocks = jnp.take(local_table, asked, axis=0)
    replies = lax.all_to_all(found_blocks, "blk", split_axis=0, concat_axis=0, tiled=True)
    fetched = replies[block_owner, position]
    pieces = []
    for slot_index in range(2 * HALF + 1):
        occupied, virtual = green_pair(fetched[slot_index * per_slot : (slot_index + 1) * per_slot])
        image = image_of(occupied, virtual, source_t)
        if slot_index == HALF:
            pieces.append(-2.0 * pair_block(partners[slot_index], image))
        else:
            pieces.append(-2.0 * split_pair_block(partners[slot_index], image))
    chi_time = jnp.concatenate(pieces, axis=1)
    column_weights = fold_weights[:, 0]
    weighted = column_weights[:, None, None] * chi_time[None]
    received = lax.all_to_all(weighted, "tau", split_axis=0, concat_axis=0, tiled=True)
    return jnp.sum(received, axis=0, keepdims=True)


def solution(mesh):
    return jax.shard_map(
        local_body,
        mesh=mesh,
        in_specs=(
            P("blk", None, None, None),
            P("tau", "blk", None),
            P("blk"),
            P("blk"),
            P(None, "tau"),
        ),
        out_specs=P("tau", "blk", None),
        check_vma=False,
    )
```

profile of v0, /device:TPU:1, one launch (start us, length us, event | category | flops | bytes accessed | tf_op | source)
XLA Modules:
  0.0 156.5 jit_solution(17804057584656822715)
XLA Ops:
  0.0 0.7 fusion.99
  0.8 0.8 select_reduce_fusion
  2.3 4.4 %scatter_fusion = s32[64,2]{0,1:T(2,128)S(1)} fusion(s32[64,2]{0,1:T(2,128)S(1)} %broadcast_in_dim.27, s32[48]{0:T(128)S(1)} %get-tuple-element.21, s32[48]{0:T(128)} %param.8), kind=kCustom, calls=%fused_computation.2 | custom fusion | bytes 960 | tf_op jit(solution)/shard_map/scatter | solution.py:77
  6.9 27.8 %all_to_all.25 = s32[64,1,2]{2,1,0:T(1,128)S(1)} all-to-all(s32[64,1,2]{2,1,0:T(1,128)S(1)} %copy.57), channel_id=1, replica_groups=mesh['tau'=8,'blk'=64] {'blk'}, dimensions={0} | all-to-all | bytes 1024 | tf_op jit(solution)/shard_map/all_to_all | solution.py:78
  35.0 0.9 gather_fusion
  36.4 1.4 broadcast_select_fusion
  37.8 4.6 %all-to-all-start.1 = ((bf16[64,2,2048]{2,1,0:T(2,128)(2,1)}), bf16[64,2,2048]{2,1,0:T(2,128)(2,1)S(1)}, u32[]{:S(2)}, u32[]{:S(2)}) async-start(bf16[64,2,2048]{2,1,0:T(2,128)(2,1)} %broadcast_select_fusion), calls=%async_computation.1 | async-start | bytes 1048576 | tf_op jit(solution)/shard_map/all_to_all | solution.py:80
  42.4 1.9 %constant_dynamic-slice_fusion.3 = (bf16[1,128,32,128]{3,2,1,0:T(8,128)(2,1)S(1)}, bf16[1,128,32,128]{3,2,1,0:T(8,128)(2,1)S(1)}) fusion(bf16[1,128,128,128]{3,2,1,0:T(8,128)(2,1)} %param.5, s32[]{:T(128)S(6)} %select_n.68, s32[]{:T(128)S(6)} %select_n.69), kind=kLoop, calls=%fused_computation.71 | loop fusion | bytes 4194312 | tf_op jit(solution)/shard_map/dynamic-slice.2
  44.4 1.7 %copy.65 = bf16[1,128,32,128]{1,3,2,0:T(8,128)(2,1)} copy(bf16[1,128,32,128]{3,2,1,0:T(8,128)(2,1)S(1)} %get-tuple-element.9) | data formatting | bytes 2097152 | tf_op jit(solution)/shard_map/dynamic-slice.2
  46.1 2.8 %collective-permute-start = (bf16[32,128,128]{1,2,0:T(8,128)(2,1)}, bf16[32,128,128]{1,2,0:T(8,128)(2,1)}, u32[]{:S(2)}, u32[]{:S(2)}) collective-permute-start(bf16[32,128,128]{1,2,0:T(8,128)(2,1)} %bitcast.124), channel_id=1, source_target_pairs={{0,1},{1,2},{2,3},{3,4},{4,5},{5,6},{6,7},{7,8},{8,9},{9,10},{10,1... | collective-permute-start | bytes 3145736 | tf_op jit(solution)/shard_map/ppermute | solution.py:14
  48.9 5.8 %collective-permute-start.4 = (bf16[32,128,128]{1,2,0:T(8,128)(2,1)}, bf16[32,128,128]{1,2,0:T(8,128)(2,1)}, u32[]{:S(2)}, u32[]{:S(2)}) collective-permute-start(bf16[32,128,128]{1,2,0:T(8,128)(2,1)} %bitcast.125), channel_id=1, source_target_pairs={{0,63},{1,0},{2,1},{3,2},{4,3},{5,4},{6,5},{7,6},{8,7},{9,8},{10,9... | collective-permute-start | bytes 3145736 | tf_op jit(solution)/shard_map/ppermute | solution.py:14
  54.7 1.0 copy.66
  55.7 1.9 %collective-permute-start.1 = (bf16[32,128,128]{1,2,0:T(8,128)(2,1)S(1)}, bf16[32,128,128]{1,2,0:T(8,128)(2,1)}, u32[]{:S(2)}, u32[]{:S(2)}) collective-permute-start(bf16[32,128,128]{1,2,0:T(8,128)(2,1)S(1)} %bitcast.126), channel_id=1, source_target_pairs={{0,1},{1,2},{2,3},{3,4},{4,5},{5,6},{6,7},{7,8},{8,9},{9,10},{10,1... | collective-permute-start | bytes 3145736 | tf_op jit(solution)/shard_map/ppermute | solution.py:14
  57.6 6.7 %collective-permute-start.5 = (bf16[32,128,128]{1,2,0:T(8,128)(2,1)S(1)}, bf16[32,128,128]{1,2,0:T(8,128)(2,1)}, u32[]{:S(2)}, u32[]{:S(2)}) collective-permute-start(bf16[32,128,128]{1,2,0:T(8,128)(2,1)S(1)} %bitcast.127), channel_id=1, source_target_pairs={{0,63},{1,0},{2,1},{3,2},{4,3},{5,4},{6,5},{7,6},{8,7},{9,8},{10,9... | collective-permute-start | bytes 3145736 | tf_op jit(solution)/shard_map/ppermute | solution.py:14
  64.3 6.8 %copy.63 = bf16[128,128,128]{2,1,0:T(8,128)(2,1)} copy(bf16[128,128,128]{0,2,1:T(8,128)(2,1)} %bitcast.122) | data formatting | bytes 8388608 | tf_op jit(solution)/shard_map/transpose | solution.py:65
  71.1 1.2 gather_fusion.1
  73.8 6.5 %fusion.19 = bf16[128,128,128]{2,1,0:T(8,128)(2,1)} fusion(bf16[128,128,1]{1,0,2:T(8,128)(2,1)S(1)} %reshape.135, bf16[128,128,1]{1,0,2:T(8,128)(2,1)S(1)} %reshape.134, bf16[128,128,128]{2,1,0:T(8,128)(2,1)} %copy.63), kind=kOutput, calls=%fused_computation.17 | convolution fusion | flops 1077936128 | bytes 8454144 | tf_op jit(solution)/shard_map/dot_general | solution.py:28
  80.3 6.5 %fusion.22 = bf16[128,128,128]{2,1,0:T(8,128)(2,1)} fusion(bf16[128,128,1]{1,0,2:T(8,128)(2,1)S(1)} %reshape.142, bf16[128,128,1]{1,0,2:T(8,128)(2,1)S(1)} %reshape.141, bf16[128,128,128]{2,1,0:T(8,128)(2,1)} %copy.63), kind=kOutput, calls=%fused_computation.18 | convolution fusion | flops 1077936128 | bytes 8454144 | tf_op jit(solution)/shard_map/dot_general | solution.py:28
  87.2 5.4 %convert_bitcast_fusion = bf16[128,128,128]{1,2,0:T(8,128)(2,1)} fusion(bf16[128,128,1]{1,0,2:T(8,128)(2,1)S(1)} %reshape.138, bf16[128,128,128]{2,1,0:T(8,128)(2,1)} %copy.63), kind=kOutput, calls=%fused_computation.13 | convolution fusion | flops 538968064 | bytes 8421376 | tf_op jit(solution)/shard_map/dot_general | solution.py:25
  92.6 12.2 %fusion.72 = f32[128,128]{0,1:T(8,128)S(1)} fusion(bf16[128,128,128]{2,0,1:T(8,128)(2,1)} %bitcast.123, bf16[128,128,1]{1,0,2:T(8,128)(2,1)S(1)} %reshape.139, bf16[128,128,128]{1,2,0:T(8,128)(2,1)} %convert_bitcast_fusion), kind=kOutput, calls=%fused_computation.44 | convolution fusion | flops 1075855360 | bytes 8486912 | tf_op jit(solution)/shard_map/dot_general | solution.py:38
  104.8 5.1 %collective-permute-start.2 = (bf16[32,128,128]{1,2,0:T(8,128)(2,1)}, bf16[32,128,128]{1,2,0:T(8,128)(2,1)S(1)}, u32[]{:S(2)}, u32[]{:S(2)}) collective-permute-start(bf16[32,128,128]{1,2,0:T(8,128)(2,1)} %collective-permute-done), channel_id=1, source_target_pairs={{0,64},{64,0},{128,192},{192,128},{256,320},{320,256},{384,448},{4... | collective-permute-start | bytes 3145736 | tf_op jit(solution)/shard_map/ppermute | solution.py:59
  109.9 1.9 %collective-permute-start.3 = (bf16[32,128,128]{1,2,0:T(8,128)(2,1)}, bf16[32,128,128]{1,2,0:T(8,128)(2,1)S(1)}, u32[]{:S(2)}, u32[]{:S(2)}) collective-permute-start(bf16[32,128,128]{1,2,0:T(8,128)(2,1)} %collective-permute-done.1), channel_id=1, source_target_pairs={{0,64},{64,0},{128,192},{192,128},{256,320},{320,256},{384,448},{4... | collective-permute-start | bytes 3145736 | tf_op jit(solution)/shard_map/ppermute | solution.py:59
  111.9 3.4 %constant_dynamic-slice_fusion.1 = (bf16[128,64,128]{2,1,0:T(8,128)(2,1)S(1)}, bf16[128,64,128]{2,1,0:T(8,128)(2,1)S(1)}) fusion(bf16[128,128,128]{2,1,0:T(8,128)(2,1)} %fusion.19, s32[]{:T(128)S(6)} %select_n.70, s32[]{:T(128)S(6)} %select_n.68), kind=kLoop, calls=%fused_computation.69 | loop fusion | bytes 8388616 | tf_op jit(solution)/shard_map/dynamic_slice | solution.py:45
  115.3 2.4 %collective-permute-start.6 = (bf16[32,128,128]{1,2,0:T(8,128)(2,1)}, bf16[32,128,128]{1,2,0:T(8,128)(2,1)S(1)}, u32[]{:S(2)}, u32[]{:S(2)}) collective-permute-start(bf16[32,128,128]{1,2,0:T(8,128)(2,1)} %collective-permute-done.4), channel_id=1, source_target_pairs={{0,64},{64,0},{128,192},{192,128},{256,320},{320,256},{384,448},{4... | collective-permute-start | bytes 3145736 | tf_op jit(solution)/shard_map/ppermute | solution.py:59
  117.7 2.2 %collective-permute-start.7 = (bf16[32,128,128]{1,2,0:T(8,128)(2,1)}, bf16[32,128,128]{1,2,0:T(8,128)(2,1)S(1)}, u32[]{:S(2)}, u32[]{:S(2)}) collective-permute-start(bf16[32,128,128]{1,2,0:T(8,128)(2,1)} %collective-permute-done.5), channel_id=1, source_target_pairs={{0,64},{64,0},{128,192},{192,128},{256,320},{320,256},{384,448},{4... | collective-permute-start | bytes 3145736 | tf_op jit(solution)/shard_map/ppermute | solution.py:59
  119.9 1.2 constant_dynamic-slice_fusion.5
  121.1 3.0 %fusion.60 = f32[128,128]{0,1:T(8,128)S(1)} fusion(bf16[32,128,128]{1,2,0:T(8,128)(2,1)} %collective-permute-done.1, bf16[32,128,128]{1,2,0:T(8,128)(2,1)} %collective-permute-done, bf16[128,64,128]{2,1,0:T(8,128)(2,1)S(1)} %get-tuple-element.6), kind=kOutput, calls=%fused_computation.42 | convolution fusion | flops 269484032 | bytes 4259840 | tf_op jit(solution)/shard_map/dot_general | solution.py:38
  124.1 3.0 %fusion.50 = f32[128,128]{0,1:T(8,128)S(1)} fusion(bf16[32,128,128]{1,2,0:T(8,128)(2,1)} %collective-permute-done.5, bf16[32,128,128]{1,2,0:T(8,128)(2,1)} %collective-permute-done.4, bf16[128,64,128]{2,1,0:T(8,128)(2,1)S(1)} %get-tuple-element.8), kind=kOutput, calls=%fused_computation.40 | convolution fusion | flops 269484032 | bytes 4259840 | tf_op jit(solution)/shard_map/dot_general | solution.py:38
  127.1 1.6 fusion.84
  128.7 1.5 fusion.94
  130.6 25.1 %all_to_all.26 = f32[8,128,384]{2,1,0:T(8,128)S(1)} all-to-all(f32[8,128,384]{2,1,0:T(8,128)S(1)} %broadcast_multiply_fusion), channel_id=1, replica_groups=mesh['tau'=8,'blk'=64] {'tau'}, dimensions={0} | all-to-all | bytes 3145728 | tf_op jit(solution)/shard_map/all_to_all | solution.py:93
  155.7 0.8 reduce_sum.19
  (46 shorter events, 3.8 us)
Async XLA Ops:
  0.0 35.0 %copy-start = (bf16[1,8,2048]{2,1,0:T(8,128)(2,1)S(1)}, bf16[1,8,2048]{2,1,0:T(8,128)(2,1)}, u32[]{:S(2)}) copy-start(bf16[1,8,2048]{2,1,0:T(8,128)(2,1)} %param.6) | copy-start | bytes 98308
  37.8 33.3 %all-to-all-start.1 = ((bf16[64,2,2048]{2,1,0:T(2,128)(2,1)}), bf16[64,2,2048]{2,1,0:T(2,128)(2,1)S(1)}, u32[]{:S(2)}, u32[]{:S(2)}) async-start(bf16[64,2,2048]{2,1,0:T(2,128)(2,1)} %broadcast_select_fusion), calls=%async_computation.1 | async-start | bytes 1048576 | tf_op jit(solution)/shard_map/all_to_all | solution.py:80
  46.1 58.7 %collective-permute-start = (bf16[32,128,128]{1,2,0:T(8,128)(2,1)}, bf16[32,128,128]{1,2,0:T(8,128)(2,1)}, u32[]{:S(2)}, u32[]{:S(2)}) collective-permute-start(bf16[32,128,128]{1,2,0:T(8,128)(2,1)} %bitcast.124), channel_id=1, source_target_pairs={{0,1},{1,2},{2,3},{3,4},{4,5},{5,6},{6,7},{7,8},{8,9},{9,10},{10,1... | collective-permute-start | bytes 3145736 | tf_op jit(solution)/shard_map/ppermute | solution.py:14
  48.9 66.4 %collective-permute-start.4 = (bf16[32,128,128]{1,2,0:T(8,128)(2,1)}, bf16[32,128,128]{1,2,0:T(8,128)(2,1)}, u32[]{:S(2)}, u32[]{:S(2)}) collective-permute-start(bf16[32,128,128]{1,2,0:T(8,128)(2,1)} %bitcast.125), channel_id=1, source_target_pairs={{0,63},{1,0},{2,1},{3,2},{4,3},{5,4},{6,5},{7,6},{8,7},{9,8},{10,9... | collective-permute-start | bytes 3145736 | tf_op jit(solution)/shard_map/ppermute | solution.py:14
  55.7 54.2 %collective-permute-start.1 = (bf16[32,128,128]{1,2,0:T(8,128)(2,1)S(1)}, bf16[32,128,128]{1,2,0:T(8,128)(2,1)}, u32[]{:S(2)}, u32[]{:S(2)}) collective-permute-start(bf16[32,128,128]{1,2,0:T(8,128)(2,1)S(1)} %bitcast.126), channel_id=1, source_target_pairs={{0,1},{1,2},{2,3},{3,4},{4,5},{5,6},{6,7},{7,8},{8,9},{9,10},{10,1... | collective-permute-start | bytes 3145736 | tf_op jit(solution)/shard_map/ppermute | solution.py:14
  57.6 60.1 %collective-permute-start.5 = (bf16[32,128,128]{1,2,0:T(8,128)(2,1)S(1)}, bf16[32,128,128]{1,2,0:T(8,128)(2,1)}, u32[]{:S(2)}, u32[]{:S(2)}) collective-permute-start(bf16[32,128,128]{1,2,0:T(8,128)(2,1)S(1)} %bitcast.127), channel_id=1, source_target_pairs={{0,63},{1,0},{2,1},{3,2},{4,3},{5,4},{6,5},{7,6},{8,7},{9,8},{10,9... | collective-permute-start | bytes 3145736 | tf_op jit(solution)/shard_map/ppermute | solution.py:14
  104.8 22.3 %collective-permute-start.2 = (bf16[32,128,128]{1,2,0:T(8,128)(2,1)}, bf16[32,128,128]{1,2,0:T(8,128)(2,1)S(1)}, u32[]{:S(2)}, u32[]{:S(2)}) collective-permute-start(bf16[32,128,128]{1,2,0:T(8,128)(2,1)} %collective-permute-done), channel_id=1, source_target_pairs={{0,64},{64,0},{128,192},{192,128},{256,320},{320,256},{384,448},{4... | collective-permute-start | bytes 3145736 | tf_op jit(solution)/shard_map/ppermute | solution.py:59
  109.9 17.2 %collective-permute-start.3 = (bf16[32,128,128]{1,2,0:T(8,128)(2,1)}, bf16[32,128,128]{1,2,0:T(8,128)(2,1)S(1)}, u32[]{:S(2)}, u32[]{:S(2)}) collective-permute-start(bf16[32,128,128]{1,2,0:T(8,128)(2,1)} %collective-permute-done.1), channel_id=1, source_target_pairs={{0,64},{64,0},{128,192},{192,128},{256,320},{320,256},{384,448},{4... | collective-permute-start | bytes 3145736 | tf_op jit(solution)/shard_map/ppermute | solution.py:59
  111.8 8.0 %copy-start.1 = (bf16[128,128,128]{2,1,0:T(8,128)(2,1)S(1)}, bf16[128,128,128]{2,1,0:T(8,128)(2,1)}, u32[]{:S(2)}) copy-start(bf16[128,128,128]{2,1,0:T(8,128)(2,1)} %fusion.22) | copy-start | bytes 12582916
  115.3 13.4 %collective-permute-start.6 = (bf16[32,128,128]{1,2,0:T(8,128)(2,1)}, bf16[32,128,128]{1,2,0:T(8,128)(2,1)S(1)}, u32[]{:S(2)}, u32[]{:S(2)}) collective-permute-start(bf16[32,128,128]{1,2,0:T(8,128)(2,1)} %collective-permute-done.4), channel_id=1, source_target_pairs={{0,64},{64,0},{128,192},{192,128},{256,320},{320,256},{384,448},{4... | collective-permute-start | bytes 3145736 | tf_op jit(solution)/shard_map/ppermute | solution.py:59
  117.7 11.0 %collective-permute-start.7 = (bf16[32,128,128]{1,2,0:T(8,128)(2,1)}, bf16[32,128,128]{1,2,0:T(8,128)(2,1)S(1)}, u32[]{:S(2)}, u32[]{:S(2)}) collective-permute-start(bf16[32,128,128]{1,2,0:T(8,128)(2,1)} %collective-permute-done.5), channel_id=1, source_target_pairs={{0,64},{64,0},{128,192},{192,128},{256,320},{320,256},{384,448},{4... | collective-permute-start | bytes 3145736 | tf_op jit(solution)/shard_map/ppermute | solution.py:59
  128.7 1.7 %copy-start.2 = (f32[8,1]{0,1:T(1,128)S(1)}, f32[8,1]{0,1:T(1,128)}, u32[]{:S(2)}) copy-start(f32[8,1]{0,1:T(1,128)} %param.9) | copy-start | bytes 100
where the time goes:
time: 157 us
  blocking collectives  52.9 us (34%)
  matrix products  39.7 us (25%)
  starting transfers between devices  33.5 us (21%)
  local copies, waits for them, and re-layouts  25.3 us (16%)
  other arithmetic  4.64 us (3%)
    all_to_all x1, blocking collectives, local_body(): lax.all_to_all(outgoing, 'blk', split_axis=0, concat_axis=0, tiled=True)  27.8 us
    all_to_all x1, blocking collectives, local_body(): lax.all_to_all(weighted, 'tau', split_axis=0, concat_axis=0, tiled=True)  25.1 us
    dot_general x5, matrix products, pair_block(): return jnp.dot(flat_image, flat_partner, preferred_element_type=jnp.float32)  21.3 us
    ppermute x4, starting transfers between devices, from_behind(): lax.ppermute(value, axis, [(i, (i + by) % size) for i in range(size)])  17.2 us
    dot_general x2, matrix products, image_of(): lax.dot_general(halfway, occupied, (((1,), (1,)), ((), ())), preferred_el...  13 us
    ppermute x4, starting transfers between devices, partner_from(): other.append(lax.ppermute(got, 'tau', [(i, i ^ 1) for i in range(size)]))  11.6 us
    transpose x1, local copies, waits for them, and re-layouts, local_body(): source_t = jnp.transpose(source, (2, 0, 1))  6.75 us
    dot_general x1, matrix products, image_of(): lax.dot_general(source_t, virtual, (((2,), (1,)), ((), ())), preferred_el...  5.37 us
  transfers between devices with their start and end apart: 9, of which 0 were waited for; matrix products, arithmetic and copies ran while one was open for 36% of the time, Pallas kernels for 0%

commit v1 on v0

--- a/solution.py
+++ b/solution.py
@@ -39,14 +39,18 @@
 
 
 def split_pair_block(halves, image):
-    core = lax.axis_index("tau") % 2
     half = image.shape[1] // 2
-    mine = lax.dynamic_slice_in_dim(image, core * half, half, 1)
-    theirs = lax.dynamic_slice_in_dim(image, (1 - core) * half, half, 1)
-    return pair_block(halves[0], mine) + pair_block(halves[1], theirs)
+    return pair_block(halves[0], image[:, :half]) + pair_block(halves[1], image[:, half:])
 
 
-def partner_from(own_t, by, chunks=2):
+def rotate_rows(virtual):
+    core = lax.axis_index("tau") % 2
+    half = virtual.shape[0] // 2
+    doubled = jnp.concatenate([virtual, virtual], axis=0)
+    return lax.dynamic_slice_in_dim(doubled, core * half, virtual.shape[0], 0)
+
+
+def partner_from(own_t, by, chunks=1):
     core = lax.axis_index("tau") % 2
     half = own_t.shape[0] // 2
     step = half // chunks
@@ -74,7 +78,10 @@
         jnp.int32
     )
     position = jnp.sum(jnp.cumsum(owner_match, axis=0) * owner_match, axis=1) - 1
-    outgoing = jnp.zeros((devices, capacity), jnp.int32).at[block_owner, position].set(block_slot)
+    place_match = (position[:, None] == jnp.arange(capacity, dtype=jnp.int32)[None, :]).astype(jnp.int32)
+    outgoing = jnp.sum(
+        owner_match[:, :, None] * place_match[:, None, :] * block_slot[:, None, None], axis=0
+    )
     asked = lax.all_to_all(outgoing, "blk", split_axis=0, concat_axis=0, tiled=True)
     found_blocks = jnp.take(local_table, asked, axis=0)
     replies = lax.all_to_all(found_blocks, "blk", split_axis=0, concat_axis=0, tiled=True)
@@ -82,6 +89,8 @@
     pieces = []
     for slot_index in range(2 * HALF + 1):
         occupied, virtual = green_pair(fetched[slot_index * per_slot : (slot_index + 1) * per_slot])
+        if slot_index != HALF:
+            virtual = rotate_rows(virtual)
         image = image_of(occupied, virtual, source_t)
         if slot_index == HALF:
             pieces.append(-2.0 * pair_block(partners[slot_index], image))

time: 157 us -> 163 us (1.038)
  waiting for transfers between devices: 0.02 us -> 15.4 us
  starting transfers between devices: 33.5 us -> 19 us
  matrix products: 39.7 us -> 44 us
    ppermute x4 -> x2, waiting for transfers between devices: 0.01 us -> 15.4 us  [from_behind(): lax.ppermute(value, axis, [(i, (i + by) % size) for i in range(size)])]
    slice x0 -> x2, local copies, waits for them, and re-layouts: none -> 9.78 us  [split_pair_block(): image[:, half:]]
    ppermute x4 -> x2, starting transfers between devices: 17.2 us -> 8.77 us  [from_behind(): lax.ppermute(value, axis, [(i, (i + by) % size) for i in range(size)])]
    ppermute x4 -> x2, starting transfers between devices: 11.6 us -> 5.58 us  [partner_from(): other.append(lax.ppermute(got, 'tau', [(i, i ^ 1) for i in range(size)]))]
    dynamic_slice x2 -> x0, local copies, waits for them, and re-layouts: 4.57 us -> none  [split_pair_block(): theirs = lax.dynamic_slice_in_dim(image, (1 - core) * half, half, 1)]
    scatter x1 -> x0, local copies, waits for them, and re-layouts: 4.45 us -> none  [local_body(): jnp.zeros((devices, capacity), jnp.int32).at[block_owner, position]]
    dot_general x5, matrix products: 21.3 us -> 25.4 us  [pair_block(): return jnp.dot(flat_image, flat_partner, preferred_element_type=jnp.float32)]
    another operation x3 -> x2, local copies, waits for them, and re-layouts: 4.62 us -> 4.71 us
  transfers between devices with their start and end apart: 9 -> 5, of which waited for: 0 -> 1; matrix products, arithmetic and copies ran while one was open for 36% -> 40% of each run, Pallas kernels for 0% -> 0%
where the time goes in v1:
time: 163 us
  blocking collectives  52.9 us (32%)
  matrix products  44 us (27%)
  local copies, waits for them, and re-layouts  26.2 us (16%)
  starting transfers between devices  19 us (12%)
  waiting for transfers between devices  15.4 us (9%)
  other arithmetic  4.77 us (3%)
    all_to_all x1, blocking collectives, local_body(): lax.all_to_all(outgoing, 'blk', split_axis=0, concat_axis=0, tiled=True)  27.8 us
    dot_general x5, matrix products, pair_block(): return jnp.dot(flat_image, flat_partner, preferred_element_type=jnp.float32)  25.4 us
    all_to_all x1, blocking collectives, local_body(): lax.all_to_all(weighted, 'tau', split_axis=0, concat_axis=0, tiled=True)  25.1 us
    ppermute x2, waiting for transfers between devices, from_behind(): lax.ppermute(value, axis, [(i, (i + by) % size) for i in range(size)])  15.4 us
    dot_general x2, matrix products, image_of(): lax.dot_general(halfway, occupied, (((1,), (1,)), ((), ())), preferred_el...  13.2 us
    slice x2, local copies, waits for them, and re-layouts, split_pair_block(): image[:, half:]  9.78 us
    ppermute x2, starting transfers between devices, from_behind(): lax.ppermute(value, axis, [(i, (i + by) % size) for i in range(size)])  8.77 us
    transpose x1, local copies, waits for them, and re-layouts, local_body(): source_t = jnp.transpose(source, (2, 0, 1))  6.72 us
  transfers between devices with their start and end apart: 5, of which 1 were waited for; matrix products, arithmetic and copies ran while one was open for 40% of the time, Pallas kernels for 0%

profile of v1, /device:TPU:1, one launch (start us, length us, event | category | flops | bytes accessed | tf_op | source)
XLA Modules:
  0.0 162.7 jit_solution(11039860593907354935)
XLA Ops:
  0.0 0.7 fusion.79
  0.8 0.8 select_reduce_fusion
  1.7 0.8 multiply_reduce_fusion
  2.5 27.8 %all_to_all.25 = s32[64,1,2]{2,1,0:T(1,128)S(1)} all-to-all(s32[64,1,2]{2,1,0:T(1,128)S(1)} %copy.54), channel_id=1, replica_groups=mesh['tau'=8,'blk'=64] {'blk'}, dimensions={0} | all-to-all | bytes 1024 | tf_op jit(solution)/shard_map/all_to_all | solution.py:85
  30.7 0.9 gather_fusion
  31.6 0.3 reshape.152
  32.1 1.4 broadcast_select_fusion
  33.5 4.6 %all-to-all-start.1 = ((bf16[64,2,2048]{2,1,0:T(2,128)(2,1)}), bf16[64,2,2048]{2,1,0:T(2,128)(2,1)S(1)}, u32[]{:S(2)}, u32[]{:S(2)}) async-start(bf16[64,2,2048]{2,1,0:T(2,128)(2,1)} %broadcast_select_fusion), calls=%async_computation.1 | async-start | bytes 1048576 | tf_op jit(solution)/shard_map/all_to_all | solution.py:87
  38.1 1.8 %constant_dynamic-slice_fusion = bf16[1,128,64,128]{3,2,1,0:T(8,128)(2,1)S(1)} fusion(bf16[1,128,128,128]{3,2,1,0:T(8,128)(2,1)} %param.5, s32[]{:T(128)S(6)} %select_n.61), kind=kLoop, calls=%fused_computation.64 | loop fusion | bytes 4194308 | tf_op jit(solution)/shard_map/dynamic-slice.1
  39.9 2.9 %copy.62 = bf16[1,128,64,128]{1,3,2,0:T(8,128)(2,1)} copy(bf16[1,128,64,128]{3,2,1,0:T(8,128)(2,1)S(1)} %constant_dynamic-slice_fusion) | data formatting | bytes 4194304 | tf_op jit(solution)/shard_map/dynamic-slice.1
  42.8 2.8 %collective-permute-start = (bf16[64,128,128]{1,2,0:T(8,128)(2,1)}, bf16[64,128,128]{1,2,0:T(8,128)(2,1)}, u32[]{:S(2)}, u32[]{:S(2)}) collective-permute-start(bf16[64,128,128]{1,2,0:T(8,128)(2,1)} %bitcast.116), channel_id=1, source_target_pairs={{0,1},{1,2},{2,3},{3,4},{4,5},{5,6},{6,7},{7,8},{8,9},{9,10},{10,1... | collective-permute-start | bytes 6291464 | tf_op jit(solution)/shard_map/ppermute | solution.py:14
  45.6 6.0 %collective-permute-start.2 = (bf16[64,128,128]{1,2,0:T(8,128)(2,1)}, bf16[64,128,128]{1,2,0:T(8,128)(2,1)}, u32[]{:S(2)}, u32[]{:S(2)}) collective-permute-start(bf16[64,128,128]{1,2,0:T(8,128)(2,1)} %bitcast.117), channel_id=1, source_target_pairs={{0,63},{1,0},{2,1},{3,2},{4,3},{5,4},{6,5},{7,6},{8,7},{9,8},{10,9... | collective-permute-start | bytes 6291464 | tf_op jit(solution)/shard_map/ppermute | solution.py:14
  51.6 6.7 %copy.60 = bf16[128,128,128]{2,1,0:T(8,128)(2,1)} copy(bf16[128,128,128]{0,2,1:T(8,128)(2,1)} %bitcast.114) | data formatting | bytes 8388608 | tf_op jit(solution)/shard_map/transpose | solution.py:69
  58.4 1.2 gather_fusion.1
  59.6 0.2 reshape.141
  60.3 0.2 reshape.148
  60.9 0.2 reshape.145
  61.1 6.6 %fusion.19 = bf16[128,128,128]{2,1,0:T(8,128)(2,1)} fusion(bf16[128,128,1]{1,0,2:T(8,128)(2,1)S(1)} %reshape.172, bf16[128,128,128]{2,1,0:T(8,128)(2,1)} %copy.60, s32[]{:T(128)S(6)} %select_n.60, bf16[128,128]{1,0:T(8,128)(2,1)S(1)} %reshape.142), kind=kOutput, calls=%fused_computation.16 | convolution fusion | flops 1078001664 | bytes 8454148 | tf_op jit(solution)/shard_map/dot_general | solution.py:28
  67.7 5.3 %fusion.94 = (bf16[128,64,128]{2,1,0:T(8,128)(2,1)}, bf16[128,64,128]{2,1,0:T(8,128)(2,1)}) fusion(bf16[128,128,128]{2,1,0:T(8,128)(2,1)} %fusion.19), kind=kLoop, calls=%fused_computation.76 | loop fusion | bytes 8388608 | tf_op jit(solution)/shard_map/slice | solution.py:43
  72.9 6.6 %fusion.22 = bf16[128,128,128]{2,1,0:T(8,128)(2,1)} fusion(bf16[128,128,1]{1,0,2:T(8,128)(2,1)S(1)} %reshape.179, bf16[128,128,128]{2,1,0:T(8,128)(2,1)} %copy.60, s32[]{:T(128)S(6)} %select_n.60, bf16[128,128]{1,0:T(8,128)(2,1)S(1)} %reshape.149), kind=kOutput, calls=%fused_computation.17 | convolution fusion | flops 1078001664 | bytes 8454148 | tf_op jit(solution)/shard_map/dot_general | solution.py:28
  79.5 4.5 %fusion.95 = (bf16[128,64,128]{2,1,0:T(8,128)(2,1)S(1)}, bf16[128,64,128]{2,1,0:T(8,128)(2,1)}) fusion(bf16[128,128,128]{2,1,0:T(8,128)(2,1)} %fusion.22), kind=kLoop, calls=%fused_computation.77 | loop fusion | bytes 8388608 | tf_op jit(solution)/shard_map/slice | solution.py:43
  84.0 15.4 %collective-permute-done = bf16[64,128,128]{1,2,0:T(8,128)(2,1)} collective-permute-done((bf16[64,128,128]{1,2,0:T(8,128)(2,1)}, bf16[64,128,128]{1,2,0:T(8,128)(2,1)}, u32[]{:S(2)}, u32[]{:S(2)}) %collective-permute-start) | collective-permute-done | bytes 2097184 | tf_op jit(solution)/shard_map/ppermute | solution.py:14
  99.4 3.4 %collective-permute-start.1 = (bf16[64,128,128]{1,2,0:T(8,128)(2,1)}, bf16[64,128,128]{1,2,0:T(8,128)(2,1)}, u32[]{:S(2)}, u32[]{:S(2)}) collective-permute-start(bf16[64,128,128]{1,2,0:T(8,128)(2,1)} %collective-permute-done), channel_id=1, source_target_pairs={{0,64},{64,0},{128,192},{192,128},{256,320},{320,256},{384,448},{4... | collective-permute-start | bytes 6291464 | tf_op jit(solution)/shard_map/ppermute | solution.py:63
  102.9 2.1 %collective-permute-start.3 = (bf16[64,128,128]{1,2,0:T(8,128)(2,1)}, bf16[64,128,128]{1,2,0:T(8,128)(2,1)}, u32[]{:S(2)}, u32[]{:S(2)}) collective-permute-start(bf16[64,128,128]{1,2,0:T(8,128)(2,1)} %collective-permute-done.2), channel_id=1, source_target_pairs={{0,64},{64,0},{128,192},{192,128},{256,320},{320,256},{384,448},{4... | collective-permute-start | bytes 6291464 | tf_op jit(solution)/shard_map/ppermute | solution.py:63
  105.5 5.4 %convert_bitcast_fusion = bf16[128,128,128]{1,2,0:T(8,128)(2,1)} fusion(bf16[128,128,1]{1,0,2:T(8,128)(2,1)S(1)} %reshape.175, bf16[128,128,128]{2,1,0:T(8,128)(2,1)} %copy.60), kind=kOutput, calls=%fused_computation.12 | convolution fusion | flops 538968064 | bytes 8421376 | tf_op jit(solution)/shard_map/dot_general | solution.py:25
  110.9 12.0 %fusion.52 = f32[128,128]{0,1:T(8,128)S(1)} fusion(bf16[128,128,128]{2,0,1:T(8,128)(2,1)} %bitcast.115, bf16[128,128,1]{1,0,2:T(8,128)(2,1)S(1)} %reshape.176, bf16[128,128,128]{1,2,0:T(8,128)(2,1)} %convert_bitcast_fusion), kind=kOutput, calls=%fused_computation.31 | convolution fusion | flops 1075855360 | bytes 8486912 | tf_op jit(solution)/shard_map/dot_general | solution.py:38
  122.9 3.8 %fusion.33 = f32[128,128]{0,1:T(8,128)S(1)} fusion(bf16[64,128,128]{1,2,0:T(8,128)(2,1)} %collective-permute-done, bf16[128,64,128]{2,1,0:T(8,128)(2,1)} %get-tuple-element.6), kind=kOutput, calls=%fused_computation.26 | convolution fusion | flops 268435456 | bytes 4259840 | tf_op jit(solution)/shard_map/dot_general | solution.py:38
  126.7 3.5 %fusion.39 = f32[128,128]{0,1:T(8,128)S(1)} fusion(bf16[64,128,128]{1,2,0:T(8,128)(2,1)} %collective-permute-done.2, bf16[128,64,128]{2,1,0:T(8,128)(2,1)S(1)} %copy-done.2), kind=kOutput, calls=%fused_computation.28 | convolution fusion | flops 268435456 | bytes 4259840 | tf_op jit(solution)/shard_map/dot_general | solution.py:38
  130.2 3.1 %fusion.68 = f32[128,128]{0,1:T(8,128)S(1)} fusion(f32[128,128]{0,1:T(8,128)S(1)} %fusion.33, bf16[64,128,128]{1,2,0:T(8,128)(2,1)} %collective-permute-done.1, bf16[128,64,128]{2,1,0:T(8,128)(2,1)S(1)} %copy-done.1), kind=kOutput, calls=%fused_computation.35 | convolution fusion | flops 268468224 | bytes 4325376 | tf_op jit(solution)/shard_map/dot_general | solution.py:38
  133.3 3.1 %fusion.62 = f32[128,128]{0,1:T(8,128)S(1)} fusion(f32[128,128]{0,1:T(8,128)S(1)} %fusion.39, bf16[64,128,128]{1,2,0:T(8,128)(2,1)} %collective-permute-done.3, bf16[128,64,128]{2,1,0:T(8,128)(2,1)S(1)} %get-tuple-element.7), kind=kOutput, calls=%fused_computation.33 | convolution fusion | flops 268468224 | bytes 4325376 | tf_op jit(solution)/shard_map/dot_general | solution.py:38
  136.8 25.1 %all_to_all.26 = f32[8,128,384]{2,1,0:T(8,128)S(1)} all-to-all(f32[8,128,384]{2,1,0:T(8,128)S(1)} %broadcast_multiply_fusion), channel_id=1, replica_groups=mesh['tau'=8,'blk'=64] {'tau'}, dimensions={0} | all-to-all | bytes 3145728 | tf_op jit(solution)/shard_map/all_to_all | solution.py:102
  161.9 0.8 reduce_sum.29
  (42 shorter events, 2.2 us)
Async XLA Ops:
  0.0 30.7 %copy-start = (bf16[1,8,2048]{2,1,0:T(8,128)(2,1)S(1)}, bf16[1,8,2048]{2,1,0:T(8,128)(2,1)}, u32[]{:S(2)}) copy-start(bf16[1,8,2048]{2,1,0:T(8,128)(2,1)} %param.6) | copy-start | bytes 98308
  33.5 24.9 %all-to-all-start.1 = ((bf16[64,2,2048]{2,1,0:T(2,128)(2,1)}), bf16[64,2,2048]{2,1,0:T(2,128)(2,1)S(1)}, u32[]{:S(2)}, u32[]{:S(2)}) async-start(bf16[64,2,2048]{2,1,0:T(2,128)(2,1)} %broadcast_select_fusion), calls=%async_computation.1 | async-start | bytes 1048576 | tf_op jit(solution)/shard_map/all_to_all | solution.py:87
  42.8 56.6 %collective-permute-start = (bf16[64,128,128]{1,2,0:T(8,128)(2,1)}, bf16[64,128,128]{1,2,0:T(8,128)(2,1)}, u32[]{:S(2)}, u32[]{:S(2)}) collective-permute-start(bf16[64,128,128]{1,2,0:T(8,128)(2,1)} %bitcast.116), channel_id=1, source_target_pairs={{0,1},{1,2},{2,3},{3,4},{4,5},{5,6},{6,7},{7,8},{8,9},{9,10},{10,1... | collective-permute-start | bytes 6291464 | tf_op jit(solution)/shard_map/ppermute | solution.py:14
  45.6 57.3 %collective-permute-start.2 = (bf16[64,128,128]{1,2,0:T(8,128)(2,1)}, bf16[64,128,128]{1,2,0:T(8,128)(2,1)}, u32[]{:S(2)}, u32[]{:S(2)}) collective-permute-start(bf16[64,128,128]{1,2,0:T(8,128)(2,1)} %bitcast.117), channel_id=1, source_target_pairs={{0,63},{1,0},{2,1},{3,2},{4,3},{5,4},{6,5},{7,6},{8,7},{9,8},{10,9... | collective-permute-start | bytes 6291464 | tf_op jit(solution)/shard_map/ppermute | solution.py:14
  51.6 6.7 %copy-start.3 = (s32[48]{0:T(128)S(1)}, s32[48]{0:T(128)}, u32[]{:S(2)}) copy-start(s32[48]{0:T(128)} %param.7) | copy-start | bytes 580
  99.4 30.7 %collective-permute-start.1 = (bf16[64,128,128]{1,2,0:T(8,128)(2,1)}, bf16[64,128,128]{1,2,0:T(8,128)(2,1)}, u32[]{:S(2)}, u32[]{:S(2)}) collective-permute-start(bf16[64,128,128]{1,2,0:T(8,128)(2,1)} %collective-permute-done), channel_id=1, source_target_pairs={{0,64},{64,0},{128,192},{192,128},{256,320},{320,256},{384,448},{4... | collective-permute-start | bytes 6291464 | tf_op jit(solution)/shard_map/ppermute | solution.py:63
  102.9 30.4 %collective-permute-start.3 = (bf16[64,128,128]{1,2,0:T(8,128)(2,1)}, bf16[64,128,128]{1,2,0:T(8,128)(2,1)}, u32[]{:S(2)}, u32[]{:S(2)}) collective-permute-start(bf16[64,128,128]{1,2,0:T(8,128)(2,1)} %collective-permute-done.2), channel_id=1, source_target_pairs={{0,64},{64,0},{128,192},{192,128},{256,320},{320,256},{384,448},{4... | collective-permute-start | bytes 6291464 | tf_op jit(solution)/shard_map/ppermute | solution.py:63
  122.9 3.8 %copy-start.2 = (bf16[128,64,128]{2,1,0:T(8,128)(2,1)S(1)}, bf16[128,64,128]{2,1,0:T(8,128)(2,1)}, u32[]{:S(2)}) copy-start(bf16[128,64,128]{2,1,0:T(8,128)(2,1)} %get-tuple-element.8) | copy-start | bytes 6291460
  126.7 3.5 %copy-start.1 = (bf16[128,64,128]{2,1,0:T(8,128)(2,1)S(1)}, bf16[128,64,128]{2,1,0:T(8,128)(2,1)}, u32[]{:S(2)}) copy-start(bf16[128,64,128]{2,1,0:T(8,128)(2,1)} %get-tuple-element.5) | copy-start | bytes 6291460
  133.3 3.3 %copy-start.4 = (f32[8,1]{0,1:T(1,128)S(1)}, f32[8,1]{0,1:T(1,128)}, u32[]{:S(2)}) copy-start(f32[8,1]{0,1:T(1,128)} %param.9) | copy-start | bytes 100

commit v2 on v0

--- a/solution.py
+++ b/solution.py
@@ -74,7 +74,10 @@
         jnp.int32
     )
     position = jnp.sum(jnp.cumsum(owner_match, axis=0) * owner_match, axis=1) - 1
-    outgoing = jnp.zeros((devices, capacity), jnp.int32).at[block_owner, position].set(block_slot)
+    place_match = (position[:, None] == jnp.arange(capacity, dtype=jnp.int32)[None, :]).astype(jnp.int32)
+    outgoing = jnp.sum(
+        owner_match[:, :, None] * place_match[:, None, :] * block_slot[:, None, None], axis=0
+    )
     asked = lax.all_to_all(outgoing, "blk", split_axis=0, concat_axis=0, tiled=True)
     found_blocks = jnp.take(local_table, asked, axis=0)
     replies = lax.all_to_all(found_blocks, "blk", split_axis=0, concat_axis=0, tiled=True)
@@ -87,11 +90,16 @@
             pieces.append(-2.0 * pair_block(partners[slot_index], image))
         else:
             pieces.append(-2.0 * split_pair_block(partners[slot_index], image))
-    chi_time = jnp.concatenate(pieces, axis=1)
-    column_weights = fold_weights[:, 0]
-    weighted = column_weights[:, None, None] * chi_time[None]
-    received = lax.all_to_all(weighted, "tau", split_axis=0, concat_axis=0, tiled=True)
-    return jnp.sum(received, axis=0, keepdims=True)
+    column_weights = fold_weights[:, 0][:, None, None]
+
+    def fold(chi):
+        received = lax.all_to_all(column_weights * chi[None], "tau", split_axis=0, concat_axis=0, tiled=True)
+        return jnp.sum(received, axis=0, keepdims=True)
+
+    own = fold(pieces[HALF])
+    sides = fold(jnp.concatenate([pieces[0], pieces[2]], axis=1))
+    width = pieces[HALF].shape[1]
+    return jnp.concatenate([sides[..., :width], own, sides[..., width:]], axis=2)
 
 
 def solution(mesh):

time: 157 us -> 162 us (1.032)
  blocking collectives: 52.9 us -> 27.8 us
  waiting for transfers between devices: 0.02 us -> 15 us
  starting transfers between devices: 33.5 us -> 43.1 us
  matrix products: 39.7 us -> 43.8 us
  other arithmetic: 4.64 us -> 6.62 us
    all_to_all x1 -> x0, blocking collectives: 25.1 us -> none  [local_body(): lax.all_to_all(weighted, 'tau', split_axis=0, concat_axis=0, tiled=True)]
    all_to_all x0 -> x2, waiting for transfers between devices: none -> 14.9 us  [fold(): lax.all_to_all(column_weights * chi[None], 'tau', split_axis=0, concat_ax...]
    all_to_all x0 -> x2, starting transfers between devices: none -> 9.6 us  [fold(): lax.all_to_all(column_weights * chi[None], 'tau', split_axis=0, concat_ax...]
    scatter x1 -> x0, local copies, waits for them, and re-layouts: 4.45 us -> none  [local_body(): jnp.zeros((devices, capacity), jnp.int32).at[block_owner, position]]
    dot_general x5, matrix products: 21.3 us -> 25.4 us  [pair_block(): return jnp.dot(flat_image, flat_partner, preferred_element_type=jnp.float32)]
    dynamic_slice x2, local copies, waits for them, and re-layouts: 4.57 us -> 7.51 us  [split_pair_block(): theirs = lax.dynamic_slice_in_dim(image, (1 - core) * half, half, 1)]
    mul x1 -> x2, other arithmetic: 0.17 us -> 2.03 us  [fold(): column_weights * chi[None]]
  transfers between devices with their start and end apart: 9 -> 11, of which waited for: 0 -> 1; matrix products, arithmetic and copies ran while one was open for 36% -> 42% of each run, Pallas kernels for 0% -> 0%
where the time goes in v2:
time: 162 us; the launch traced here: 161 us
  matrix products  43.8 us (27%)
  starting transfers between devices  43.1 us (27%)
  blocking collectives  27.8 us (17%)
  local copies, waits for them, and re-layouts  23.9 us (15%)
  waiting for transfers between devices  15 us (9%)
  other arithmetic  6.62 us (4%)
    all_to_all x1, blocking collectives, local_body(): lax.all_to_all(outgoing, 'blk', split_axis=0, concat_axis=0, tiled=True)  27.8 us
    dot_general x5, matrix products, pair_block(): return jnp.dot(flat_image, flat_partner, preferred_element_type=jnp.float32)  25.4 us
    ppermute x4, starting transfers between devices, from_behind(): lax.ppermute(value, axis, [(i, (i + by) % size) for i in range(size)])  17.2 us
    all_to_all x2, waiting for transfers between devices, fold(): lax.all_to_all(column_weights * chi[None], 'tau', split_axis=0, concat_ax...  14.9 us
    dot_general x2, matrix products, image_of(): lax.dot_general(halfway, occupied, (((1,), (1,)), ((), ())), preferred_el...  13 us
    ppermute x4, starting transfers between devices, partner_from(): other.append(lax.ppermute(got, 'tau', [(i, i ^ 1) for i in range(size)]))  11.6 us
    all_to_all x2, starting transfers between devices, fold(): lax.all_to_all(column_weights * chi[None], 'tau', split_axis=0, concat_ax...  9.6 us
    dynamic_slice x2, local copies, waits for them, and re-layouts, split_pair_block(): theirs = lax.dynamic_slice_in_dim(image, (1 - core) * half, half, 1)  7.51 us
  transfers between devices with their start and end apart: 11, of which 1 were waited for; matrix products, arithmetic and copies ran while one was open for 42% of the time, Pallas kernels for 0%

profile of v2, /device:TPU:1, one launch (start us, length us, event | category | flops | bytes accessed | tf_op | source)
XLA Modules:
  0.0 160.6 jit_solution(1314206994330572854)
XLA Ops:
  2.5 27.8 %all_to_all.30 = s32[64,1,2]{2,1,0:T(1,128)S(1)} all-to-all(s32[64,1,2]{2,1,0:T(1,128)S(1)} %copy.63), channel_id=1, replica_groups=mesh['tau'=8,'blk'=64] {'blk'}, dimensions={0} | all-to-all | bytes 1024 | tf_op jit(solution)/shard_map/all_to_all | solution.py:81
  30.7 0.9 gather_fusion
  32.1 1.4 broadcast_select_fusion
  33.4 4.6 %all-to-all-start.1 = ((bf16[64,2,2048]{2,1,0:T(2,128)(2,1)}), bf16[64,2,2048]{2,1,0:T(2,128)(2,1)S(1)}, u32[]{:S(2)}, u32[]{:S(2)}) async-start(bf16[64,2,2048]{2,1,0:T(2,128)(2,1)} %broadcast_select_fusion), calls=%async_computation.1 | async-start | bytes 1048576 | tf_op jit(solution)/shard_map/all_to_all | solution.py:83
  38.1 1.9 %constant_dynamic-slice_fusion.3 = (bf16[1,128,32,128]{3,2,1,0:T(8,128)(2,1)S(1)}, bf16[1,128,32,128]{3,2,1,0:T(8,128)(2,1)S(1)}) fusion(bf16[1,128,128,128]{3,2,1,0:T(8,128)(2,1)} %param.5, s32[]{:T(128)S(6)} %select_n.66, s32[]{:T(128)S(6)} %select_n.67), kind=kLoop, calls=%fused_computation.73 | loop fusion | bytes 4194312 | tf_op jit(solution)/shard_map/dynamic-slice.2
  40.0 1.7 %copy.71 = bf16[1,128,32,128]{1,3,2,0:T(8,128)(2,1)} copy(bf16[1,128,32,128]{3,2,1,0:T(8,128)(2,1)S(1)} %get-tuple-element.9) | data formatting | bytes 2097152 | tf_op jit(solution)/shard_map/dynamic-slice.2
  41.7 2.8 %collective-permute-start = (bf16[32,128,128]{1,2,0:T(8,128)(2,1)}, bf16[32,128,128]{1,2,0:T(8,128)(2,1)}, u32[]{:S(2)}, u32[]{:S(2)}) collective-permute-start(bf16[32,128,128]{1,2,0:T(8,128)(2,1)} %bitcast.110), channel_id=1, source_target_pairs={{0,1},{1,2},{2,3},{3,4},{4,5},{5,6},{6,7},{7,8},{8,9},{9,10},{10,1... | collective-permute-start | bytes 3145736 | tf_op jit(solution)/shard_map/ppermute | solution.py:14
  44.5 5.8 %collective-permute-start.4 = (bf16[32,128,128]{1,2,0:T(8,128)(2,1)}, bf16[32,128,128]{1,2,0:T(8,128)(2,1)}, u32[]{:S(2)}, u32[]{:S(2)}) collective-permute-start(bf16[32,128,128]{1,2,0:T(8,128)(2,1)} %bitcast.111), channel_id=1, source_target_pairs={{0,63},{1,0},{2,1},{3,2},{4,3},{5,4},{6,5},{7,6},{8,7},{9,8},{10,9... | collective-permute-start | bytes 3145736 | tf_op jit(solution)/shard_map/ppermute | solution.py:14
  50.3 1.0 copy.72
  51.3 1.9 %collective-permute-start.1 = (bf16[32,128,128]{1,2,0:T(8,128)(2,1)S(1)}, bf16[32,128,128]{1,2,0:T(8,128)(2,1)}, u32[]{:S(2)}, u32[]{:S(2)}) collective-permute-start(bf16[32,128,128]{1,2,0:T(8,128)(2,1)S(1)} %bitcast.112), channel_id=1, source_target_pairs={{0,1},{1,2},{2,3},{3,4},{4,5},{5,6},{6,7},{7,8},{8,9},{9,10},{10,1... | collective-permute-start | bytes 3145736 | tf_op jit(solution)/shard_map/ppermute | solution.py:14
  53.3 6.7 %collective-permute-start.5 = (bf16[32,128,128]{1,2,0:T(8,128)(2,1)S(1)}, bf16[32,128,128]{1,2,0:T(8,128)(2,1)}, u32[]{:S(2)}, u32[]{:S(2)}) collective-permute-start(bf16[32,128,128]{1,2,0:T(8,128)(2,1)S(1)} %bitcast.113), channel_id=1, source_target_pairs={{0,63},{1,0},{2,1},{3,2},{4,3},{5,4},{6,5},{7,6},{8,7},{9,8},{10,9... | collective-permute-start | bytes 3145736 | tf_op jit(solution)/shard_map/ppermute | solution.py:14
  60.0 6.8 %copy.69 = bf16[128,128,128]{2,1,0:T(8,128)(2,1)} copy(bf16[128,128,128]{0,2,1:T(8,128)(2,1)} %bitcast.108) | data formatting | bytes 8388608 | tf_op jit(solution)/shard_map/transpose | solution.py:65
  66.8 1.2 gather_fusion.1
  69.9 5.4 %convert_bitcast_fusion = bf16[128,128,128]{1,2,0:T(8,128)(2,1)} fusion(bf16[128,128,1]{1,0,2:T(8,128)(2,1)S(1)} %reshape.184, bf16[128,128,128]{2,1,0:T(8,128)(2,1)} %copy.69), kind=kOutput, calls=%fused_computation.11 | convolution fusion | flops 538968064 | bytes 8421376 | tf_op jit(solution)/shard_map/dot_general | solution.py:25
  75.3 12.2 %fusion.72 = f32[128,128]{0,1:T(8,128)S(1)} fusion(bf16[128,128,128]{2,0,1:T(8,128)(2,1)} %bitcast.109, bf16[128,128,1]{1,0,2:T(8,128)(2,1)S(1)} %reshape.185, bf16[128,128,128]{1,2,0:T(8,128)(2,1)} %convert_bitcast_fusion), kind=kOutput, calls=%fused_computation.43 | convolution fusion | flops 1075855360 | bytes 8486912 | tf_op jit(solution)/shard_map/dot_general | solution.py:38
  87.6 0.9 broadcast_multiply_fusion.1
  88.5 6.5 %fusion.19 = bf16[128,128,128]{2,1,0:T(8,128)(2,1)} fusion(bf16[128,128,1]{1,0,2:T(8,128)(2,1)S(1)} %reshape.177, bf16[128,128,1]{1,0,2:T(8,128)(2,1)S(1)} %reshape.176, bf16[128,128,128]{2,1,0:T(8,128)(2,1)} %copy.69), kind=kOutput, calls=%fused_computation.16 | convolution fusion | flops 1077936128 | bytes 8454144 | tf_op jit(solution)/shard_map/dot_general | solution.py:28
  95.0 6.5 %fusion.22 = bf16[128,128,128]{2,1,0:T(8,128)(2,1)} fusion(bf16[128,128,1]{1,0,2:T(8,128)(2,1)S(1)} %reshape.181, bf16[128,128,1]{1,0,2:T(8,128)(2,1)S(1)} %reshape.180, bf16[128,128,128]{2,1,0:T(8,128)(2,1)} %copy.69), kind=kOutput, calls=%fused_computation.17 | convolution fusion | flops 1077936128 | bytes 8454144 | tf_op jit(solution)/shard_map/dot_general | solution.py:28
  101.5 5.4 %collective-permute-start.2 = (bf16[32,128,128]{1,2,0:T(8,128)(2,1)}, bf16[32,128,128]{1,2,0:T(8,128)(2,1)}, u32[]{:S(2)}, u32[]{:S(2)}) collective-permute-start(bf16[32,128,128]{1,2,0:T(8,128)(2,1)} %collective-permute-done), channel_id=1, source_target_pairs={{0,64},{64,0},{128,192},{192,128},{256,320},{320,256},{384,448},{4... | collective-permute-start | bytes 3145736 | tf_op jit(solution)/shard_map/ppermute | solution.py:59
  107.0 1.9 %collective-permute-start.3 = (bf16[32,128,128]{1,2,0:T(8,128)(2,1)}, bf16[32,128,128]{1,2,0:T(8,128)(2,1)}, u32[]{:S(2)}, u32[]{:S(2)}) collective-permute-start(bf16[32,128,128]{1,2,0:T(8,128)(2,1)} %collective-permute-done.1), channel_id=1, source_target_pairs={{0,64},{64,0},{128,192},{192,128},{256,320},{320,256},{384,448},{4... | collective-permute-start | bytes 3145736 | tf_op jit(solution)/shard_map/ppermute | solution.py:59
  108.9 4.6 %constant_dynamic-slice_fusion.1 = (bf16[128,64,128]{2,1,0:T(8,128)(2,1)S(1)}, bf16[128,64,128]{2,1,0:T(8,128)(2,1)}) fusion(bf16[128,128,128]{2,1,0:T(8,128)(2,1)} %fusion.19, s32[]{:T(128)S(6)} %select_n.68, s32[]{:T(128)S(6)} %select_n.66), kind=kLoop, calls=%fused_computation.71 | loop fusion | bytes 8388616 | tf_op jit(solution)/shard_map/dynamic_slice | solution.py:45
  113.5 2.4 %collective-permute-start.6 = (bf16[32,128,128]{1,2,0:T(8,128)(2,1)}, bf16[32,128,128]{1,2,0:T(8,128)(2,1)}, u32[]{:S(2)}, u32[]{:S(2)}) collective-permute-start(bf16[32,128,128]{1,2,0:T(8,128)(2,1)} %collective-permute-done.4), channel_id=1, source_target_pairs={{0,64},{64,0},{128,192},{192,128},{256,320},{320,256},{384,448},{4... | collective-permute-start | bytes 3145736 | tf_op jit(solution)/shard_map/ppermute | solution.py:59
  115.9 1.9 %collective-permute-start.7 = (bf16[32,128,128]{1,2,0:T(8,128)(2,1)}, bf16[32,128,128]{1,2,0:T(8,128)(2,1)}, u32[]{:S(2)}, u32[]{:S(2)}) collective-permute-start(bf16[32,128,128]{1,2,0:T(8,128)(2,1)} %collective-permute-done.5), channel_id=1, source_target_pairs={{0,64},{64,0},{128,192},{192,128},{256,320},{320,256},{384,448},{4... | collective-permute-start | bytes 3145736 | tf_op jit(solution)/shard_map/ppermute | solution.py:59
  117.8 2.9 %constant_dynamic-slice_fusion.5 = (bf16[128,64,128]{2,1,0:T(8,128)(2,1)}, bf16[128,64,128]{2,1,0:T(8,128)(2,1)}) fusion(bf16[128,128,128]{2,1,0:T(8,128)(2,1)S(1)} %copy-done.1, s32[]{:T(128)S(6)} %select_n.68, s32[]{:T(128)S(6)} %select_n.66), kind=kLoop, calls=%fused_computation.75 | loop fusion | bytes 8388616 | tf_op jit(solution)/shard_map/dynamic_slice | solution.py:45
  120.8 4.8 %all-to-all-start.3 = ((f32[8,128,128]{2,1,0:T(8,128)}), f32[8,128,128]{2,1,0:T(8,128)S(1)}, u32[]{:S(2)}, u32[]{:S(2)}) async-start(f32[8,128,128]{2,1,0:T(8,128)} %broadcast_multiply_fusion.1), calls=%async_computation.3 | async-start | bytes 1048576 | tf_op jit(solution)/shard_map/all_to_all | solution.py:96
  125.6 3.7 %fusion.60 = f32[128,128]{0,1:T(8,128)S(1)} fusion(bf16[32,128,128]{1,2,0:T(8,128)(2,1)} %collective-permute-done.1, bf16[32,128,128]{1,2,0:T(8,128)(2,1)} %collective-permute-done, bf16[128,64,128]{2,1,0:T(8,128)(2,1)} %get-tuple-element.6), kind=kOutput, calls=%fused_computation.41 | convolution fusion | flops 269484032 | bytes 4259840 | tf_op jit(solution)/shard_map/dot_general | solution.py:38
  129.3 3.1 %fusion.50 = f32[128,128]{0,1:T(8,128)S(1)} fusion(bf16[32,128,128]{1,2,0:T(8,128)(2,1)} %collective-permute-done.5, bf16[32,128,128]{1,2,0:T(8,128)(2,1)} %collective-permute-done.4, bf16[128,64,128]{2,1,0:T(8,128)(2,1)S(1)} %copy-done.3), kind=kOutput, calls=%fused_computation.39 | convolution fusion | flops 269484032 | bytes 4259840 | tf_op jit(solution)/shard_map/dot_general | solution.py:38
  132.5 3.2 %fusion.84 = f32[128,128]{0,1:T(8,128)S(1)} fusion(f32[128,128]{0,1:T(8,128)S(1)} %fusion.60, bf16[32,128,128]{1,2,0:T(8,128)(2,1)} %collective-permute-done.3, bf16[32,128,128]{1,2,0:T(8,128)(2,1)} %collective-permute-done.2, bf16[128,64,128]{2,1,0:T(8,128)(2,1)S(1)} %get-tuple-element.5), kind=kOutput, calls=%fused_computation.45 | convolution fusion | flops 269516800 | bytes 4325376 | tf_op jit(solution)/shard_map/dot_general | solution.py:38
  135.7 3.1 %fusion.94 = f32[128,128]{0,1:T(8,128)S(1)} fusion(f32[128,128]{0,1:T(8,128)S(1)} %fusion.50, bf16[32,128,128]{1,2,0:T(8,128)(2,1)} %collective-permute-done.7, bf16[32,128,128]{1,2,0:T(8,128)(2,1)} %collective-permute-done.6, bf16[128,64,128]{2,1,0:T(8,128)(2,1)S(1)} %copy-done.2), kind=kOutput, calls=%fused_computation.47 | convolution fusion | flops 269516800 | bytes 4325376 | tf_op jit(solution)/shard_map/dot_general | solution.py:38
  138.9 1.1 broadcast_multiply_fusion
  140.1 4.8 %all-to-all-start.2 = ((f32[8,128,256]{2,1,0:T(8,128)}), f32[8,128,256]{2,1,0:T(8,128)S(1)}, u32[]{:S(2)}, u32[]{:S(2)}) async-start(f32[8,128,256]{2,1,0:T(8,128)} %broadcast_multiply_fusion), calls=%async_computation.2 | async-start | bytes 2097152 | tf_op jit(solution)/shard_map/all_to_all | solution.py:96
  144.9 14.9 %all-to-all-done.2 = f32[8,128,256]{2,1,0:T(8,128)S(1)} async-done(((f32[8,128,256]{2,1,0:T(8,128)}), f32[8,128,256]{2,1,0:T(8,128)S(1)}, u32[]{:S(2)}, u32[]{:S(2)}) %all-to-all-start.2) | async-done | bytes 1048608 | tf_op jit(solution)/shard_map/all_to_all | solution.py:96
  (61 shorter events, 6.1 us)
Async XLA Ops:
  0.0 30.7 %copy-start = (bf16[1,8,2048]{2,1,0:T(8,128)(2,1)S(1)}, bf16[1,8,2048]{2,1,0:T(8,128)(2,1)}, u32[]{:S(2)}) copy-start(bf16[1,8,2048]{2,1,0:T(8,128)(2,1)} %param.6) | copy-start | bytes 98308
  33.4 33.3 %all-to-all-start.1 = ((bf16[64,2,2048]{2,1,0:T(2,128)(2,1)}), bf16[64,2,2048]{2,1,0:T(2,128)(2,1)S(1)}, u32[]{:S(2)}, u32[]{:S(2)}) async-start(bf16[64,2,2048]{2,1,0:T(2,128)(2,1)} %broadcast_select_fusion), calls=%async_computation.1 | async-start | bytes 1048576 | tf_op jit(solution)/shard_map/all_to_all | solution.py:83
  41.7 59.8 %collective-permute-start = (bf16[32,128,128]{1,2,0:T(8,128)(2,1)}, bf16[32,128,128]{1,2,0:T(8,128)(2,1)}, u32[]{:S(2)}, u32[]{:S(2)}) collective-permute-start(bf16[32,128,128]{1,2,0:T(8,128)(2,1)} %bitcast.110), channel_id=1, source_target_pairs={{0,1},{1,2},{2,3},{3,4},{4,5},{5,6},{6,7},{7,8},{8,9},{9,10},{10,1... | collective-permute-start | bytes 3145736 | tf_op jit(solution)/shard_map/ppermute | solution.py:14
  44.5 68.9 %collective-permute-start.4 = (bf16[32,128,128]{1,2,0:T(8,128)(2,1)}, bf16[32,128,128]{1,2,0:T(8,128)(2,1)}, u32[]{:S(2)}, u32[]{:S(2)}) collective-permute-start(bf16[32,128,128]{1,2,0:T(8,128)(2,1)} %bitcast.111), channel_id=1, source_target_pairs={{0,63},{1,0},{2,1},{3,2},{4,3},{5,4},{6,5},{7,6},{8,7},{9,8},{10,9... | collective-permute-start | bytes 3145736 | tf_op jit(solution)/shard_map/ppermute | solution.py:14
  51.3 55.6 %collective-permute-start.1 = (bf16[32,128,128]{1,2,0:T(8,128)(2,1)S(1)}, bf16[32,128,128]{1,2,0:T(8,128)(2,1)}, u32[]{:S(2)}, u32[]{:S(2)}) collective-permute-start(bf16[32,128,128]{1,2,0:T(8,128)(2,1)S(1)} %bitcast.112), channel_id=1, source_target_pairs={{0,1},{1,2},{2,3},{3,4},{4,5},{5,6},{6,7},{7,8},{8,9},{9,10},{10,1... | collective-permute-start | bytes 3145736 | tf_op jit(solution)/shard_map/ppermute | solution.py:14
  53.3 62.6 %collective-permute-start.5 = (bf16[32,128,128]{1,2,0:T(8,128)(2,1)S(1)}, bf16[32,128,128]{1,2,0:T(8,128)(2,1)}, u32[]{:S(2)}, u32[]{:S(2)}) collective-permute-start(bf16[32,128,128]{1,2,0:T(8,128)(2,1)S(1)} %bitcast.113), channel_id=1, source_target_pairs={{0,63},{1,0},{2,1},{3,2},{4,3},{5,4},{6,5},{7,6},{8,7},{9,8},{10,9... | collective-permute-start | bytes 3145736 | tf_op jit(solution)/shard_map/ppermute | solution.py:14
  60.0 6.8 %copy-start.4 = (s32[48]{0:T(128)S(1)}, s32[48]{0:T(128)}, u32[]{:S(2)}) copy-start(s32[48]{0:T(128)} %param.7) | copy-start | bytes 580
  75.3 12.3 %copy-start.5 = (f32[8,1]{0,1:T(1,128)S(1)}, f32[8,1]{0,1:T(1,128)}, u32[]{:S(2)}) copy-start(f32[8,1]{0,1:T(1,128)} %param.9) | copy-start | bytes 100
  101.5 16.3 %copy-start.1 = (bf16[128,128,128]{2,1,0:T(8,128)(2,1)S(1)}, bf16[128,128,128]{2,1,0:T(8,128)(2,1)}, u32[]{:S(2)}) copy-start(bf16[128,128,128]{2,1,0:T(8,128)(2,1)} %fusion.22) | copy-start | bytes 12582916
  101.5 30.9 %collective-permute-start.2 = (bf16[32,128,128]{1,2,0:T(8,128)(2,1)}, bf16[32,128,128]{1,2,0:T(8,128)(2,1)}, u32[]{:S(2)}, u32[]{:S(2)}) collective-permute-start(bf16[32,128,128]{1,2,0:T(8,128)(2,1)} %collective-permute-done), channel_id=1, source_target_pairs={{0,64},{64,0},{128,192},{192,128},{256,320},{320,256},{384,448},{4... | collective-permute-start | bytes 3145736 | tf_op jit(solution)/shard_map/ppermute | solution.py:59
  107.0 25.5 %collective-permute-start.3 = (bf16[32,128,128]{1,2,0:T(8,128)(2,1)}, bf16[32,128,128]{1,2,0:T(8,128)(2,1)}, u32[]{:S(2)}, u32[]{:S(2)}) collective-permute-start(bf16[32,128,128]{1,2,0:T(8,128)(2,1)} %collective-permute-done.1), channel_id=1, source_target_pairs={{0,64},{64,0},{128,192},{192,128},{256,320},{320,256},{384,448},{4... | collective-permute-start | bytes 3145736 | tf_op jit(solution)/shard_map/ppermute | solution.py:59
  113.5 22.2 %collective-permute-start.6 = (bf16[32,128,128]{1,2,0:T(8,128)(2,1)}, bf16[32,128,128]{1,2,0:T(8,128)(2,1)}, u32[]{:S(2)}, u32[]{:S(2)}) collective-permute-start(bf16[32,128,128]{1,2,0:T(8,128)(2,1)} %collective-permute-done.4), channel_id=1, source_target_pairs={{0,64},{64,0},{128,192},{192,128},{256,320},{320,256},{384,448},{4... | collective-permute-start | bytes 3145736 | tf_op jit(solution)/shard_map/ppermute | solution.py:59
  115.9 19.8 %collective-permute-start.7 = (bf16[32,128,128]{1,2,0:T(8,128)(2,1)}, bf16[32,128,128]{1,2,0:T(8,128)(2,1)}, u32[]{:S(2)}, u32[]{:S(2)}) collective-permute-start(bf16[32,128,128]{1,2,0:T(8,128)(2,1)} %collective-permute-done.5), channel_id=1, source_target_pairs={{0,64},{64,0},{128,192},{192,128},{256,320},{320,256},{384,448},{4... | collective-permute-start | bytes 3145736 | tf_op jit(solution)/shard_map/ppermute | solution.py:59
  120.8 19.3 %all-to-all-start.3 = ((f32[8,128,128]{2,1,0:T(8,128)}), f32[8,128,128]{2,1,0:T(8,128)S(1)}, u32[]{:S(2)}, u32[]{:S(2)}) async-start(f32[8,128,128]{2,1,0:T(8,128)} %broadcast_multiply_fusion.1), calls=%async_computation.3 | async-start | bytes 1048576 | tf_op jit(solution)/shard_map/all_to_all | solution.py:96
  125.6 3.8 %copy-start.3 = (bf16[128,64,128]{2,1,0:T(8,128)(2,1)S(1)}, bf16[128,64,128]{2,1,0:T(8,128)(2,1)}, u32[]{:S(2)}) copy-start(bf16[128,64,128]{2,1,0:T(8,128)(2,1)} %get-tuple-element.8) | copy-start | bytes 6291460
  132.4 3.3 %copy-start.2 = (bf16[128,64,128]{2,1,0:T(8,128)(2,1)S(1)}, bf16[128,64,128]{2,1,0:T(8,128)(2,1)}, u32[]{:S(2)}) copy-start(bf16[128,64,128]{2,1,0:T(8,128)(2,1)} %get-tuple-element.7) | copy-start | bytes 6291460
  140.1 19.8 %all-to-all-start.2 = ((f32[8,128,256]{2,1,0:T(8,128)}), f32[8,128,256]{2,1,0:T(8,128)S(1)}, u32[]{:S(2)}, u32[]{:S(2)}) async-start(f32[8,128,256]{2,1,0:T(8,128)} %broadcast_multiply_fusion), calls=%async_computation.2 | async-start | bytes 2097152 | tf_op jit(solution)/shard_map/all_to_all | solution.py:96

commit v3 on v0

--- a/solution.py
+++ b/solution.py
@@ -74,7 +74,10 @@
         jnp.int32
     )
     position = jnp.sum(jnp.cumsum(owner_match, axis=0) * owner_match, axis=1) - 1
-    outgoing = jnp.zeros((devices, capacity), jnp.int32).at[block_owner, position].set(block_slot)
+    place_match = (position[:, None] == jnp.arange(capacity, dtype=jnp.int32)[None, :]).astype(jnp.int32)
+    outgoing = jnp.sum(
+        owner_match[:, :, None] * place_match[:, None, :] * block_slot[:, None, None], axis=0
+    )
     asked = lax.all_to_all(outgoing, "blk", split_axis=0, concat_axis=0, tiled=True)
     found_blocks = jnp.take(local_table, asked, axis=0)
     replies = lax.all_to_all(found_blocks, "blk", split_axis=0, concat_axis=0, tiled=True)
@@ -84,7 +87,9 @@
         occupied, virtual = green_pair(fetched[slot_index * per_slot : (slot_index + 1) * per_slot])
         image = image_of(occupied, virtual, source_t)
         if slot_index == HALF:
-            pieces.append(-2.0 * pair_block(partners[slot_index], image))
+            half = image.shape[1] // 2
+            own_part = pair_block(own_t[:half], image[:, :half]) + pair_block(own_t[half:], image[:, half:])
+            pieces.append(-2.0 * own_part)
         else:
             pieces.append(-2.0 * split_pair_block(partners[slot_index], image))
     chi_time = jnp.concatenate(pieces, axis=1)

time: 157 us -> 160 us (1.019)
  local copies, waits for them, and re-layouts: 25.3 us -> 32.3 us
  matrix products: 39.7 us -> 35.6 us
    unnamed x6 -> x9, local copies, waits for them, and re-layouts: 0.01 us -> 6.93 us
    dot_general x2 -> x3, matrix products: 13 us -> 19.8 us  [image_of(): lax.dot_general(halfway, occupied, (((1,), (1,)), ((), ())), preferred_el...]
    dot_general x5 -> x6, matrix products: 21.3 us -> 15.8 us  [pair_block(): return jnp.dot(flat_image, flat_partner, preferred_element_type=jnp.float32)]
    dot_general x1 -> x0, matrix products: 5.37 us -> none  [image_of(): lax.dot_general(source_t, virtual, (((2,), (1,)), ((), ())), preferred_el...]
    slice x0 -> x1, local copies, waits for them, and re-layouts: none -> 4.54 us  [local_body(): image[:, half:]]
    scatter x1 -> x0, local copies, waits for them, and re-layouts: 4.45 us -> none  [local_body(): jnp.zeros((devices, capacity), jnp.int32).at[block_owner, position]]
  transfers between devices with their start and end apart: 9 -> 9, of which waited for: 0 -> 0; matrix products, arithmetic and copies ran while one was open for 36% -> 40% of each run, Pallas kernels for 0% -> 0%
where the time goes in v3:
time: 160 us; the launch traced here: 159 us
  blocking collectives  52.9 us (33%)
  matrix products  35.6 us (22%)
  starting transfers between devices  33.2 us (21%)
  local copies, waits for them, and re-layouts  32.3 us (20%)
  other arithmetic  4.78 us (3%)
    all_to_all x1, blocking collectives, local_body(): lax.all_to_all(outgoing, 'blk', split_axis=0, concat_axis=0, tiled=True)  27.8 us
    all_to_all x1, blocking collectives, local_body(): lax.all_to_all(weighted, 'tau', split_axis=0, concat_axis=0, tiled=True)  25.2 us
    dot_general x3, matrix products, image_of(): lax.dot_general(halfway, occupied, (((1,), (1,)), ((), ())), preferred_el...  19.8 us
    ppermute x4, starting transfers between devices, from_behind(): lax.ppermute(value, axis, [(i, (i + by) % size) for i in range(size)])  17.2 us
    dot_general x6, matrix products, pair_block(): return jnp.dot(flat_image, flat_partner, preferred_element_type=jnp.float32)  15.8 us
    ppermute x4, starting transfers between devices, partner_from(): other.append(lax.ppermute(got, 'tau', [(i, i ^ 1) for i in range(size)]))  11.4 us
    unnamed x9, local copies, waits for them, and re-layouts  6.93 us
    transpose x1, local copies, waits for them, and re-layouts, local_body(): source_t = jnp.transpose(source, (2, 0, 1))  6.69 us
  transfers between devices with their start and end apart: 9, of which 0 were waited for; matrix products, arithmetic and copies ran while one was open for 40% of the time, Pallas kernels for 0%

profile of v3, /device:TPU:1, one launch (start us, length us, event | category | flops | bytes accessed | tf_op | source)
XLA Modules:
  0.0 159.2 jit_solution(8996733441320207940)
XLA Ops:
  0.8 0.8 select_reduce_fusion
  2.5 27.8 %all_to_all.25 = s32[64,1,2]{2,1,0:T(1,128)S(1)} all-to-all(s32[64,1,2]{2,1,0:T(1,128)S(1)} %copy.63), channel_id=1, replica_groups=mesh['tau'=8,'blk'=64] {'blk'}, dimensions={0} | all-to-all | bytes 1024 | tf_op jit(solution)/shard_map/all_to_all | solution.py:81
  30.7 0.9 gather_fusion
  32.1 1.4 broadcast_select_fusion
  33.5 4.6 %all-to-all-start.1 = ((bf16[64,2,2048]{2,1,0:T(2,128)(2,1)}), bf16[64,2,2048]{2,1,0:T(2,128)(2,1)S(1)}, u32[]{:S(2)}, u32[]{:S(2)}) async-start(bf16[64,2,2048]{2,1,0:T(2,128)(2,1)} %broadcast_select_fusion), calls=%async_computation.1 | async-start | bytes 1048576 | tf_op jit(solution)/shard_map/all_to_all | solution.py:83
  38.1 1.9 %constant_dynamic-slice_fusion.3 = (bf16[1,128,32,128]{3,2,1,0:T(8,128)(2,1)S(1)}, bf16[1,128,32,128]{3,2,1,0:T(8,128)(2,1)S(1)}) fusion(bf16[1,128,128,128]{3,2,1,0:T(8,128)(2,1)} %param.5, s32[]{:T(128)S(6)} %select_n.66, s32[]{:T(128)S(6)} %select_n.67), kind=kLoop, calls=%fused_computation.78 | loop fusion | bytes 4194312 | tf_op jit(solution)/shard_map/dynamic-slice.2
  40.1 1.7 %copy.72 = bf16[1,128,32,128]{1,3,2,0:T(8,128)(2,1)} copy(bf16[1,128,32,128]{3,2,1,0:T(8,128)(2,1)S(1)} %get-tuple-element.11) | data formatting | bytes 2097152 | tf_op jit(solution)/shard_map/dynamic-slice.2
  41.8 2.8 %collective-permute-start = (bf16[32,128,128]{1,2,0:T(8,128)(2,1)}, bf16[32,128,128]{1,2,0:T(8,128)(2,1)}, u32[]{:S(2)}, u32[]{:S(2)}) collective-permute-start(bf16[32,128,128]{1,2,0:T(8,128)(2,1)} %bitcast.120), channel_id=1, source_target_pairs={{0,1},{1,2},{2,3},{3,4},{4,5},{5,6},{6,7},{7,8},{8,9},{9,10},{10,1... | collective-permute-start | bytes 3145736 | tf_op jit(solution)/shard_map/ppermute | solution.py:14
  44.6 5.8 %collective-permute-start.4 = (bf16[32,128,128]{1,2,0:T(8,128)(2,1)}, bf16[32,128,128]{1,2,0:T(8,128)(2,1)}, u32[]{:S(2)}, u32[]{:S(2)}) collective-permute-start(bf16[32,128,128]{1,2,0:T(8,128)(2,1)} %bitcast.121), channel_id=1, source_target_pairs={{0,63},{1,0},{2,1},{3,2},{4,3},{5,4},{6,5},{7,6},{8,7},{9,8},{10,9... | collective-permute-start | bytes 3145736 | tf_op jit(solution)/shard_map/ppermute | solution.py:14
  50.4 1.0 copy.73
  51.4 1.9 %collective-permute-start.1 = (bf16[32,128,128]{1,2,0:T(8,128)(2,1)S(1)}, bf16[32,128,128]{1,2,0:T(8,128)(2,1)}, u32[]{:S(2)}, u32[]{:S(2)}) collective-permute-start(bf16[32,128,128]{1,2,0:T(8,128)(2,1)S(1)} %bitcast.122), channel_id=1, source_target_pairs={{0,1},{1,2},{2,3},{3,4},{4,5},{5,6},{6,7},{7,8},{8,9},{9,10},{10,1... | collective-permute-start | bytes 3145736 | tf_op jit(solution)/shard_map/ppermute | solution.py:14
  53.3 6.7 %collective-permute-start.5 = (bf16[32,128,128]{1,2,0:T(8,128)(2,1)S(1)}, bf16[32,128,128]{1,2,0:T(8,128)(2,1)}, u32[]{:S(2)}, u32[]{:S(2)}) collective-permute-start(bf16[32,128,128]{1,2,0:T(8,128)(2,1)S(1)} %bitcast.123), channel_id=1, source_target_pairs={{0,63},{1,0},{2,1},{3,2},{4,3},{5,4},{6,5},{7,6},{8,7},{9,8},{10,9... | collective-permute-start | bytes 3145736 | tf_op jit(solution)/shard_map/ppermute | solution.py:14
  60.0 6.9 %copy.69 = bf16[1,128,128,128]{1,3,2,0:T(8,128)(2,1)} copy(bf16[1,128,128,128]{3,2,1,0:T(8,128)(2,1)} %param.5) | data formatting | bytes 8388608 | tf_op args[0]
  66.9 6.7 %copy.70 = bf16[128,128,128]{2,1,0:T(8,128)(2,1)} copy(bf16[128,128,128]{0,2,1:T(8,128)(2,1)} %bitcast.117) | data formatting | bytes 8388608 | tf_op jit(solution)/shard_map/transpose | solution.py:65
  73.6 1.2 gather_fusion.1
  76.3 6.5 %fusion.18 = bf16[128,128,128]{2,1,0:T(8,128)(2,1)} fusion(bf16[128,128,1]{1,0,2:T(8,128)(2,1)S(1)} %reshape.182, bf16[128,128,1]{1,0,2:T(8,128)(2,1)S(1)} %reshape.181, bf16[128,128,128]{2,1,0:T(8,128)(2,1)} %copy.70), kind=kOutput, calls=%fused_computation.15 | convolution fusion | flops 1077936128 | bytes 8454144 | tf_op jit(solution)/shard_map/dot_general | solution.py:28
  82.8 4.5 %fusion.121 = (bf16[128,64,128]{2,1,0:T(8,128)(2,1)S(1)}, bf16[128,64,128]{2,1,0:T(8,128)(2,1)}) fusion(bf16[128,128,128]{2,1,0:T(8,128)(2,1)} %fusion.18), kind=kLoop, calls=%fused_computation.92 | loop fusion | bytes 8388608 | tf_op jit(solution)/shard_map/slice | solution.py:91
  87.4 6.5 %fusion.15 = bf16[128,128,128]{2,1,0:T(8,128)(2,1)} fusion(bf16[128,128,1]{1,0,2:T(8,128)(2,1)S(1)} %reshape.178, bf16[128,128,1]{1,0,2:T(8,128)(2,1)S(1)} %reshape.177, bf16[128,128,128]{2,1,0:T(8,128)(2,1)} %copy.70), kind=kOutput, calls=%fused_computation.14 | convolution fusion | flops 1077936128 | bytes 8454144 | tf_op jit(solution)/shard_map/dot_general | solution.py:28
  93.9 3.6 %fusion.70 = f32[128,128]{0,1:T(8,128)S(1)} fusion(bf16[128,128,128]{1,2,0:T(8,128)(2,1)} %bitcast.118, bf16[128,64,128]{2,1,0:T(8,128)(2,1)} %get-tuple-element.8), kind=kOutput, calls=%fused_computation.47 | convolution fusion | flops 268435456 | bytes 4259840 | tf_op jit(solution)/shard_map/dot_general | solution.py:38
  98.0 3.0 %fusion.105 = f32[128,128]{0,1:T(8,128)S(1)} fusion(f32[128,128]{0,1:T(8,128)S(1)} %fusion.70, bf16[128,128,128]{1,2,0:T(8,128)(2,1)} %bitcast.119, bf16[128,64,128]{2,1,0:T(8,128)(2,1)S(1)} %get-tuple-element.7), kind=kOutput, calls=%fused_computation.54 | convolution fusion | flops 268468224 | bytes 4325376 | tf_op jit(solution)/shard_map/dot_general | solution.py:38
  101.0 6.8 %fusion.21 = bf16[128,128,128]{2,1,0:T(8,128)(2,1)} fusion(bf16[128,128,1]{1,0,2:T(8,128)(2,1)S(1)} %reshape.186, bf16[128,128,1]{1,0,2:T(8,128)(2,1)S(1)} %reshape.185, bf16[128,128,128]{2,1,0:T(8,128)(2,1)} %copy.70), kind=kOutput, calls=%fused_computation.16 | convolution fusion | flops 1077936128 | bytes 8454144 | tf_op jit(solution)/shard_map/dot_general | solution.py:28
  107.8 5.1 %collective-permute-start.2 = (bf16[32,128,128]{1,2,0:T(8,128)(2,1)}, bf16[32,128,128]{1,2,0:T(8,128)(2,1)S(1)}, u32[]{:S(2)}, u32[]{:S(2)}) collective-permute-start(bf16[32,128,128]{1,2,0:T(8,128)(2,1)} %collective-permute-done), channel_id=1, source_target_pairs={{0,64},{64,0},{128,192},{192,128},{256,320},{320,256},{384,448},{4... | collective-permute-start | bytes 3145736 | tf_op jit(solution)/shard_map/ppermute | solution.py:59
  112.9 1.9 %collective-permute-start.3 = (bf16[32,128,128]{1,2,0:T(8,128)(2,1)}, bf16[32,128,128]{1,2,0:T(8,128)(2,1)S(1)}, u32[]{:S(2)}, u32[]{:S(2)}) collective-permute-start(bf16[32,128,128]{1,2,0:T(8,128)(2,1)} %collective-permute-done.1), channel_id=1, source_target_pairs={{0,64},{64,0},{128,192},{192,128},{256,320},{320,256},{384,448},{4... | collective-permute-start | bytes 3145736 | tf_op jit(solution)/shard_map/ppermute | solution.py:59
  114.9 3.4 %constant_dynamic-slice_fusion.1 = (bf16[128,64,128]{2,1,0:T(8,128)(2,1)S(1)}, bf16[128,64,128]{2,1,0:T(8,128)(2,1)S(1)}) fusion(bf16[128,128,128]{2,1,0:T(8,128)(2,1)} %fusion.15, s32[]{:T(128)S(6)} %select_n.68, s32[]{:T(128)S(6)} %select_n.66), kind=kLoop, calls=%fused_computation.76 | loop fusion | bytes 8388616 | tf_op jit(solution)/shard_map/dynamic_slice | solution.py:45
  118.3 2.4 %collective-permute-start.6 = (bf16[32,128,128]{1,2,0:T(8,128)(2,1)}, bf16[32,128,128]{1,2,0:T(8,128)(2,1)S(1)}, u32[]{:S(2)}, u32[]{:S(2)}) collective-permute-start(bf16[32,128,128]{1,2,0:T(8,128)(2,1)} %collective-permute-done.4), channel_id=1, source_target_pairs={{0,64},{64,0},{128,192},{192,128},{256,320},{320,256},{384,448},{4... | collective-permute-start | bytes 3145736 | tf_op jit(solution)/shard_map/ppermute | solution.py:59
  120.7 1.9 %collective-permute-start.7 = (bf16[32,128,128]{1,2,0:T(8,128)(2,1)}, bf16[32,128,128]{1,2,0:T(8,128)(2,1)S(1)}, u32[]{:S(2)}, u32[]{:S(2)}) collective-permute-start(bf16[32,128,128]{1,2,0:T(8,128)(2,1)} %collective-permute-done.5), channel_id=1, source_target_pairs={{0,64},{64,0},{128,192},{192,128},{256,320},{320,256},{384,448},{4... | collective-permute-start | bytes 3145736 | tf_op jit(solution)/shard_map/ppermute | solution.py:59
  122.6 1.2 constant_dynamic-slice_fusion.5
  123.8 3.0 %fusion.65 = f32[128,128]{0,1:T(8,128)S(1)} fusion(bf16[32,128,128]{1,2,0:T(8,128)(2,1)} %collective-permute-done.1, bf16[32,128,128]{1,2,0:T(8,128)(2,1)} %collective-permute-done, bf16[128,64,128]{2,1,0:T(8,128)(2,1)S(1)} %get-tuple-element.6), kind=kOutput, calls=%fused_computation.46 | convolution fusion | flops 269484032 | bytes 4259840 | tf_op jit(solution)/shard_map/dot_general | solution.py:38
  126.8 3.0 %fusion.55 = f32[128,128]{0,1:T(8,128)S(1)} fusion(bf16[32,128,128]{1,2,0:T(8,128)(2,1)} %collective-permute-done.5, bf16[32,128,128]{1,2,0:T(8,128)(2,1)} %collective-permute-done.4, bf16[128,64,128]{2,1,0:T(8,128)(2,1)S(1)} %get-tuple-element.10), kind=kOutput, calls=%fused_computation.44 | convolution fusion | flops 269484032 | bytes 4259840 | tf_op jit(solution)/shard_map/dot_general | solution.py:38
  129.8 1.6 fusion.90
  131.4 1.5 fusion.100
  133.3 25.2 %all_to_all.26 = f32[8,128,384]{2,1,0:T(8,128)S(1)} all-to-all(f32[8,128,384]{2,1,0:T(8,128)S(1)} %broadcast_multiply_fusion), channel_id=1, replica_groups=mesh['tau'=8,'blk'=64] {'tau'}, dimensions={0} | all-to-all | bytes 3145728 | tf_op jit(solution)/shard_map/all_to_all | solution.py:98
  (52 shorter events, 5.4 us)
Async XLA Ops:
  0.0 30.7 %copy-start = (bf16[1,8,2048]{2,1,0:T(8,128)(2,1)S(1)}, bf16[1,8,2048]{2,1,0:T(8,128)(2,1)}, u32[]{:S(2)}) copy-start(bf16[1,8,2048]{2,1,0:T(8,128)(2,1)} %param.6) | copy-start | bytes 98308
  33.5 40.1 %all-to-all-start.1 = ((bf16[64,2,2048]{2,1,0:T(2,128)(2,1)}), bf16[64,2,2048]{2,1,0:T(2,128)(2,1)S(1)}, u32[]{:S(2)}, u32[]{:S(2)}) async-start(bf16[64,2,2048]{2,1,0:T(2,128)(2,1)} %broadcast_select_fusion), calls=%async_computation.1 | async-start | bytes 1048576 | tf_op jit(solution)/shard_map/all_to_all | solution.py:83
  41.8 66.0 %collective-permute-start = (bf16[32,128,128]{1,2,0:T(8,128)(2,1)}, bf16[32,128,128]{1,2,0:T(8,128)(2,1)}, u32[]{:S(2)}, u32[]{:S(2)}) collective-permute-start(bf16[32,128,128]{1,2,0:T(8,128)(2,1)} %bitcast.120), channel_id=1, source_target_pairs={{0,1},{1,2},{2,3},{3,4},{4,5},{5,6},{6,7},{7,8},{8,9},{9,10},{10,1... | collective-permute-start | bytes 3145736 | tf_op jit(solution)/shard_map/ppermute | solution.py:14
  44.6 73.7 %collective-permute-start.4 = (bf16[32,128,128]{1,2,0:T(8,128)(2,1)}, bf16[32,128,128]{1,2,0:T(8,128)(2,1)}, u32[]{:S(2)}, u32[]{:S(2)}) collective-permute-start(bf16[32,128,128]{1,2,0:T(8,128)(2,1)} %bitcast.121), channel_id=1, source_target_pairs={{0,63},{1,0},{2,1},{3,2},{4,3},{5,4},{6,5},{7,6},{8,7},{9,8},{10,9... | collective-permute-start | bytes 3145736 | tf_op jit(solution)/shard_map/ppermute | solution.py:14
  51.4 61.5 %collective-permute-start.1 = (bf16[32,128,128]{1,2,0:T(8,128)(2,1)S(1)}, bf16[32,128,128]{1,2,0:T(8,128)(2,1)}, u32[]{:S(2)}, u32[]{:S(2)}) collective-permute-start(bf16[32,128,128]{1,2,0:T(8,128)(2,1)S(1)} %bitcast.122), channel_id=1, source_target_pairs={{0,1},{1,2},{2,3},{3,4},{4,5},{5,6},{6,7},{7,8},{8,9},{9,10},{10,1... | collective-permute-start | bytes 3145736 | tf_op jit(solution)/shard_map/ppermute | solution.py:14
  53.3 67.4 %collective-permute-start.5 = (bf16[32,128,128]{1,2,0:T(8,128)(2,1)S(1)}, bf16[32,128,128]{1,2,0:T(8,128)(2,1)}, u32[]{:S(2)}, u32[]{:S(2)}) collective-permute-start(bf16[32,128,128]{1,2,0:T(8,128)(2,1)S(1)} %bitcast.123), channel_id=1, source_target_pairs={{0,63},{1,0},{2,1},{3,2},{4,3},{5,4},{6,5},{7,6},{8,7},{9,8},{10,9... | collective-permute-start | bytes 3145736 | tf_op jit(solution)/shard_map/ppermute | solution.py:14
  66.9 6.7 %copy-start.2 = (s32[48]{0:T(128)S(1)}, s32[48]{0:T(128)}, u32[]{:S(2)}) copy-start(s32[48]{0:T(128)} %param.7) | copy-start | bytes 580
  107.8 22.1 %collective-permute-start.2 = (bf16[32,128,128]{1,2,0:T(8,128)(2,1)}, bf16[32,128,128]{1,2,0:T(8,128)(2,1)S(1)}, u32[]{:S(2)}, u32[]{:S(2)}) collective-permute-start(bf16[32,128,128]{1,2,0:T(8,128)(2,1)} %collective-permute-done), channel_id=1, source_target_pairs={{0,64},{64,0},{128,192},{192,128},{256,320},{320,256},{384,448},{4... | collective-permute-start | bytes 3145736 | tf_op jit(solution)/shard_map/ppermute | solution.py:59
  112.9 16.9 %collective-permute-start.3 = (bf16[32,128,128]{1,2,0:T(8,128)(2,1)}, bf16[32,128,128]{1,2,0:T(8,128)(2,1)S(1)}, u32[]{:S(2)}, u32[]{:S(2)}) collective-permute-start(bf16[32,128,128]{1,2,0:T(8,128)(2,1)} %collective-permute-done.1), channel_id=1, source_target_pairs={{0,64},{64,0},{128,192},{192,128},{256,320},{320,256},{384,448},{4... | collective-permute-start | bytes 3145736 | tf_op jit(solution)/shard_map/ppermute | solution.py:59
  114.8 7.8 %copy-start.1 = (bf16[128,128,128]{2,1,0:T(8,128)(2,1)S(1)}, bf16[128,128,128]{2,1,0:T(8,128)(2,1)}, u32[]{:S(2)}) copy-start(bf16[128,128,128]{2,1,0:T(8,128)(2,1)} %fusion.21) | copy-start | bytes 12582916
  118.3 13.2 %collective-permute-start.6 = (bf16[32,128,128]{1,2,0:T(8,128)(2,1)}, bf16[32,128,128]{1,2,0:T(8,128)(2,1)S(1)}, u32[]{:S(2)}, u32[]{:S(2)}) collective-permute-start(bf16[32,128,128]{1,2,0:T(8,128)(2,1)} %collective-permute-done.4), channel_id=1, source_target_pairs={{0,64},{64,0},{128,192},{192,128},{256,320},{320,256},{384,448},{4... | collective-permute-start | bytes 3145736 | tf_op jit(solution)/shard_map/ppermute | solution.py:59
  120.7 10.7 %collective-permute-start.7 = (bf16[32,128,128]{1,2,0:T(8,128)(2,1)}, bf16[32,128,128]{1,2,0:T(8,128)(2,1)S(1)}, u32[]{:S(2)}, u32[]{:S(2)}) collective-permute-start(bf16[32,128,128]{1,2,0:T(8,128)(2,1)} %collective-permute-done.5), channel_id=1, source_target_pairs={{0,64},{64,0},{128,192},{192,128},{256,320},{320,256},{384,448},{4... | collective-permute-start | bytes 3145736 | tf_op jit(solution)/shard_map/ppermute | solution.py:59
  131.4 1.7 %copy-start.3 = (f32[8,1]{0,1:T(1,128)S(1)}, f32[8,1]{0,1:T(1,128)}, u32[]{:S(2)}) copy-start(f32[8,1]{0,1:T(1,128)} %param.9) | copy-start | bytes 100

commit v4 on v3

--- a/solution.py
+++ b/solution.py
@@ -46,25 +46,32 @@
     return pair_block(halves[0], mine) + pair_block(halves[1], theirs)
 
 
-def partner_from(own_t, by, chunks=2):
+def partners_from(own_t, chunks=2):
     core = lax.axis_index("tau") % 2
     half = own_t.shape[0] // 2
     step = half // chunks
     size = lax.axis_size("tau")
-    fetched, other = [], []
+    fetched, other = {-1: [], 1: []}, {-1: [], 1: []}
     for k in range(chunks):
         mine = lax.dynamic_slice_in_dim(own_t, core * half + k * step, step, 0)
-        got = from_behind(mine, "blk", by)
-        fetched.append(got)
-        other.append(lax.ppermute(got, "tau", [(i, i ^ 1) for i in range(size)]))
-    return jnp.concatenate(fetched, axis=0), jnp.concatenate(other, axis=0)
+        got = {}
+        for by in (1, -1):
+            got[by] = from_behind(mine, "blk", by)
+        swapped = lax.ppermute(jnp.stack([got[1], got[-1]]), "tau", [(i, i ^ 1) for i in range(size)])
+        for n, by in enumerate((1, -1)):
+            fetched[by].append(got[by])
+            other[by].append(swapped[n])
+    return {
+        by: (jnp.concatenate(fetched[by], axis=0), jnp.concatenate(other[by], axis=0)) for by in (1, -1)
+    }
 
 
 def local_body(three_center, green_blocks, block_owner, block_slot, fold_weights):
     source = three_center[0]
     source_t = jnp.transpose(source, (2, 0, 1))
     own_t = jnp.transpose(source, (1, 0, 2))
-    partners = [partner_from(own_t, HALF - j) if j != HALF else own_t for j in range(2 * HALF + 1)]
+    neighbours = partners_from(own_t)
+    partners = [neighbours[HALF - j] if j != HALF else own_t for j in range(2 * HALF + 1)]
     local_table = green_blocks[0]
     devices = lax.axis_size("blk")
     requests = block_owner.shape[0]
@@ -87,9 +94,7 @@
         occupied, virtual = green_pair(fetched[slot_index * per_slot : (slot_index + 1) * per_slot])
         image = image_of(occupied, virtual, source_t)
         if slot_index == HALF:
-            half = image.shape[1] // 2
-            own_part = pair_block(own_t[:half], image[:, :half]) + pair_block(own_t[half:], image[:, half:])
-            pieces.append(-2.0 * own_part)
+            pieces.append(-2.0 * pair_block(partners[slot_index], image))
         else:
             pieces.append(-2.0 * split_pair_block(partners[slot_index], image))
     chi_time = jnp.concatenate(pieces, axis=1)

time: 160 us -> 177 us (1.11)
  waiting for transfers between devices: 0.02 us -> 15.1 us
  other arithmetic: 4.78 us -> 11.1 us
  local copies, waits for them, and re-layouts: 32.3 us -> 28 us
  starting transfers between devices: 33.2 us -> 31 us
  matrix products: 35.6 us -> 37.7 us
    ppermute x4, waiting for transfers between devices: 0.01 us -> 15.1 us  [from_behind(): lax.ppermute(value, axis, [(i, (i + by) % size) for i in range(size)])]
    dot_general x3 -> x2, matrix products: 19.8 us -> 13.1 us  [image_of(): lax.dot_general(halfway, occupied, (((1,), (1,)), ((), ())), preferred_el...]
    unnamed x9 -> x16, local copies, waits for them, and re-layouts: 6.93 us -> 0.55 us
    another operation x0 -> x2, other arithmetic: none -> 6.34 us  [partners_from(): jnp.stack([got[1], got[-1]])]
    dot_general x6 -> x5, matrix products: 15.8 us -> 21.4 us  [pair_block(): return jnp.dot(flat_image, flat_partner, preferred_element_type=jnp.float32)]
    slice x1 -> x0, local copies, waits for them, and re-layouts: 4.54 us -> none  [local_body(): image[:, half:]]
    squeeze x0 -> x2, local copies, waits for them, and re-layouts: none -> 3.5 us  [partners_from(): other[by].append(swapped[n])]
    dot_general x0 -> x1, matrix products: none -> 3.23 us  [image_of(): lax.dot_general(source_t, virtual, (((2,), (1,)), ((), ())), preferred_el...]
  transfers between devices with their start and end apart: 9 -> 7, of which waited for: 0 -> 2; matrix products, arithmetic and copies ran while one was open for 40% -> 33% of each run, Pallas kernels for 0% -> 0%
where the time goes in v4:
time: 177 us; the launch traced here: 176 us
  blocking collectives  52.6 us (30%)
  matrix products  37.7 us (21%)
  starting transfers between devices  31 us (18%)
  local copies, waits for them, and re-layouts  28 us (16%)
  waiting for transfers between devices  15.1 us (9%)
  other arithmetic  11.1 us (6%)
    all_to_all x1, blocking collectives, local_body(): lax.all_to_all(outgoing, 'blk', split_axis=0, concat_axis=0, tiled=True)  27.8 us
    all_to_all x1, blocking collectives, local_body(): lax.all_to_all(weighted, 'tau', split_axis=0, concat_axis=0, tiled=True)  24.8 us
    dot_general x5, matrix products, pair_block(): return jnp.dot(flat_image, flat_partner, preferred_element_type=jnp.float32)  21.4 us
    ppermute x4, starting transfers between devices, from_behind(): lax.ppermute(value, axis, [(i, (i + by) % size) for i in range(size)])  17.2 us
    ppermute x4, waiting for transfers between devices, from_behind(): lax.ppermute(value, axis, [(i, (i + by) % size) for i in range(size)])  15.1 us
    dot_general x2, matrix products, image_of(): lax.dot_general(halfway, occupied, (((1,), (1,)), ((), ())), preferred_el...  13.1 us
    ppermute x2, starting transfers between devices, partners_from(): lax.ppermute(jnp.stack([got[1], got[-1]]), 'tau', [(i, i ^ 1) for i in ra...  9.14 us
    dynamic_slice x2, local copies, waits for them, and re-layouts, split_pair_block(): mine = lax.dynamic_slice_in_dim(image, core * half, half, 1)  7.66 us
  transfers between devices with their start and end apart: 7, of which 2 were waited for; matrix products, arithmetic and copies ran while one was open for 33% of the time, Pallas kernels for 0%

profile of v4, /device:TPU:1, one launch (start us, length us, event | category | flops | bytes accessed | tf_op | source)
XLA Modules:
  0.0 175.8 jit_solution(171776472898712416)
XLA Ops:
  2.5 27.8 %all_to_all.25 = s32[64,1,2]{2,1,0:T(1,128)S(1)} all-to-all(s32[64,1,2]{2,1,0:T(1,128)S(1)} %copy.57), channel_id=1, replica_groups=mesh['tau'=8,'blk'=64] {'blk'}, dimensions={0} | all-to-all | bytes 1024 | tf_op jit(solution)/shard_map/all_to_all | solution.py:88
  30.7 0.9 gather_fusion
  32.1 1.4 broadcast_select_fusion
  33.4 4.6 %all-to-all-start.1 = ((bf16[64,2,2048]{2,1,0:T(2,128)(2,1)}), bf16[64,2,2048]{2,1,0:T(2,128)(2,1)S(1)}, u32[]{:S(2)}, u32[]{:S(2)}) async-start(bf16[64,2,2048]{2,1,0:T(2,128)(2,1)} %broadcast_select_fusion), calls=%async_computation.1 | async-start | bytes 1048576 | tf_op jit(solution)/shard_map/all_to_all | solution.py:90
  38.1 1.9 %constant_dynamic-slice_fusion.3 = (bf16[1,128,32,128]{3,2,1,0:T(8,128)(2,1)S(1)}, bf16[1,128,32,128]{3,2,1,0:T(8,128)(2,1)S(1)}) fusion(bf16[1,128,128,128]{3,2,1,0:T(8,128)(2,1)} %param.5, s32[]{:T(128)S(6)} %select_n.62, s32[]{:T(128)S(6)} %select_n.63), kind=kLoop, calls=%fused_computation.77 | loop fusion | bytes 4194312 | tf_op jit(solution)/shard_map/dynamic-slice.2
  40.0 1.7 copy.65
  41.8 2.8 %collective-permute-start = (bf16[32,128,128]{1,2,0:T(8,128)(2,1)}, bf16[32,128,128]{1,2,0:T(8,128)(2,1)}, u32[]{:S(2)}, u32[]{:S(2)}) collective-permute-start(bf16[32,128,128]{1,2,0:T(8,128)(2,1)} %bitcast.123), channel_id=1, source_target_pairs={{0,1},{1,2},{2,3},{3,4},{4,5},{5,6},{6,7},{7,8},{8,9},{9,10},{10,1... | collective-permute-start | bytes 3145736 | tf_op jit(solution)/shard_map/ppermute | solution.py:14
  44.6 5.8 %collective-permute-start.2 = (bf16[32,128,128]{1,2,0:T(8,128)(2,1)}, bf16[32,128,128]{1,2,0:T(8,128)(2,1)}, u32[]{:S(2)}, u32[]{:S(2)}) collective-permute-start(bf16[32,128,128]{1,2,0:T(8,128)(2,1)} %bitcast.124), channel_id=1, source_target_pairs={{0,63},{1,0},{2,1},{3,2},{4,3},{5,4},{6,5},{7,6},{8,7},{9,8},{10,9... | collective-permute-start | bytes 3145736 | tf_op jit(solution)/shard_map/ppermute | solution.py:14
  50.4 1.0 copy.66
  51.4 1.9 %collective-permute-start.1 = (bf16[32,128,128]{1,2,0:T(8,128)(2,1)S(1)}, bf16[32,128,128]{1,2,0:T(8,128)(2,1)}, u32[]{:S(2)}, u32[]{:S(2)}) collective-permute-start(bf16[32,128,128]{1,2,0:T(8,128)(2,1)S(1)} %bitcast.121), channel_id=1, source_target_pairs={{0,1},{1,2},{2,3},{3,4},{4,5},{5,6},{6,7},{7,8},{8,9},{9,10},{10,1... | collective-permute-start | bytes 3145736 | tf_op jit(solution)/shard_map/ppermute | solution.py:14
  53.3 6.7 %collective-permute-start.4 = (bf16[32,128,128]{1,2,0:T(8,128)(2,1)S(1)}, bf16[32,128,128]{1,2,0:T(8,128)(2,1)}, u32[]{:S(2)}, u32[]{:S(2)}) collective-permute-start(bf16[32,128,128]{1,2,0:T(8,128)(2,1)S(1)} %bitcast.122), channel_id=1, source_target_pairs={{0,63},{1,0},{2,1},{3,2},{4,3},{5,4},{6,5},{7,6},{8,7},{9,8},{10,9... | collective-permute-start | bytes 3145736 | tf_op jit(solution)/shard_map/ppermute | solution.py:14
  60.0 6.7 %copy.63 = bf16[128,128,128]{2,1,0:T(8,128)(2,1)} copy(bf16[128,128,128]{0,2,1:T(8,128)(2,1)} %bitcast.119) | data formatting | bytes 8388608 | tf_op jit(solution)/shard_map/transpose | solution.py:71
  66.8 1.2 gather_fusion.1
  69.2 6.5 %fusion.19 = bf16[128,128,128]{2,1,0:T(8,128)(2,1)} fusion(bf16[128,128,1]{1,0,2:T(8,128)(2,1)S(1)} %reshape.176, bf16[128,128,1]{1,0,2:T(8,128)(2,1)S(1)} %reshape.175, bf16[128,128,128]{2,1,0:T(8,128)(2,1)} %copy.63), kind=kOutput, calls=%fused_computation.16 | convolution fusion | flops 1077936128 | bytes 8454144 | tf_op jit(solution)/shard_map/dot_general | solution.py:28
  75.7 1.0 collective-permute-done
  76.8 3.1 %pad_maximum_fusion = bf16[2,32,128,128]{2,3,1,0:T(8,128)(2,1)} fusion(bf16[1,32,128,128]{2,3,1,0:T(8,128)(2,1)} %bitcast.23, bf16[1,32,128,128]{2,3,1,0:T(8,128)(2,1)} %bitcast.21), kind=kLoop, calls=%fused_computation.22 | loop fusion | flops 1048576 | bytes 4194304 | tf_op jit(solution)/shard_map/stack | solution.py:60
  79.8 5.2 %collective-permute-start.3 = (bf16[2,32,128,128]{2,3,1,0:T(8,128)(2,1)}, bf16[2,32,128,128]{2,3,1,0:T(8,128)(2,1)}, u32[]{:S(2)}, u32[]{:S(2)}) collective-permute-start(bf16[2,32,128,128]{2,3,1,0:T(8,128)(2,1)} %pad_maximum_fusion), channel_id=1, source_target_pairs={{0,64},{64,0},{128,192},{192,128},{256,320},{320,256},{384,448},{4... | collective-permute-start | bytes 6291464 | tf_op jit(solution)/shard_map/ppermute | solution.py:60
  85.2 14.0 %collective-permute-done.1 = bf16[32,128,128]{1,2,0:T(8,128)(2,1)} collective-permute-done((bf16[32,128,128]{1,2,0:T(8,128)(2,1)S(1)}, bf16[32,128,128]{1,2,0:T(8,128)(2,1)}, u32[]{:S(2)}, u32[]{:S(2)}) %collective-permute-start.1) | collective-permute-done | bytes 1048608 | tf_op jit(solution)/shard_map/ppermute | solution.py:14
  99.2 3.3 %pad_maximum_fusion.1 = bf16[2,32,128,128]{2,3,1,0:T(8,128)(2,1)} fusion(bf16[1,32,128,128]{2,3,1,0:T(8,128)(2,1)} %bitcast.27, bf16[1,32,128,128]{2,3,1,0:T(8,128)(2,1)} %bitcast.25), kind=kLoop, calls=%fused_computation.23 | loop fusion | flops 1048576 | bytes 4194304 | tf_op jit(solution)/shard_map/stack | solution.py:60
  102.5 4.0 %collective-permute-start.5 = (bf16[2,32,128,128]{2,3,1,0:T(8,128)(2,1)}, bf16[2,32,128,128]{2,3,1,0:T(8,128)(2,1)}, u32[]{:S(2)}, u32[]{:S(2)}) collective-permute-start(bf16[2,32,128,128]{2,3,1,0:T(8,128)(2,1)} %pad_maximum_fusion.1), channel_id=1, source_target_pairs={{0,64},{64,0},{128,192},{192,128},{256,320},{320,256},{384,448},{4... | collective-permute-start | bytes 6291464 | tf_op jit(solution)/shard_map/ppermute | solution.py:60
  106.5 2.3 %constant_dynamic-slice_fusion.4 = (bf16[128,64,128]{2,1,0:T(8,128)(2,1)S(1)}, bf16[128,64,128]{2,1,0:T(8,128)(2,1)}) fusion(bf16[128,128,128]{2,1,0:T(8,128)(2,1)S(1)} %copy-done.2, s32[]{:T(128)S(6)} %select_n.62, s32[]{:T(128)S(6)} %select_n.64), kind=kLoop, calls=%fused_computation.78 | loop fusion | bytes 8388616 | tf_op jit(solution)/shard_map/dynamic_slice | solution.py:44
  109.3 6.5 %fusion.22 = bf16[128,128,128]{2,1,0:T(8,128)(2,1)} fusion(bf16[128,128,1]{1,0,2:T(8,128)(2,1)S(1)} %reshape.183, bf16[128,128,1]{1,0,2:T(8,128)(2,1)S(1)} %reshape.182, bf16[128,128,128]{2,1,0:T(8,128)(2,1)} %copy.63), kind=kOutput, calls=%fused_computation.17 | convolution fusion | flops 1077936128 | bytes 8454144 | tf_op jit(solution)/shard_map/dot_general | solution.py:28
  115.8 5.4 %constant_dynamic-slice_fusion = (bf16[128,64,128]{2,1,0:T(8,128)(2,1)}, bf16[128,64,128]{2,1,0:T(8,128)(2,1)}) fusion(bf16[128,128,128]{2,1,0:T(8,128)(2,1)} %fusion.22, s32[]{:T(128)S(6)} %select_n.62, s32[]{:T(128)S(6)} %select_n.64), kind=kLoop, calls=%fused_computation.74 | loop fusion | bytes 8388616 | tf_op jit(solution)/shard_map/dynamic_slice | solution.py:44
  121.2 3.2 %convert_bitcast_fusion = bf16[128,128,128]{1,2,0:T(8,128)(2,1)} fusion(bf16[128,128,1]{1,0,2:T(8,128)(2,1)S(1)} %reshape.179, bf16[128,128,128]{2,1,0:T(8,128)(2,1)S(1)} %copy-done.1), kind=kOutput, calls=%fused_computation.12 | convolution fusion | flops 538968064 | bytes 8421376 | tf_op jit(solution)/shard_map/dot_general | solution.py:25
  124.4 12.2 %fusion.72 = f32[128,128]{0,1:T(8,128)S(1)} fusion(bf16[128,128,128]{2,0,1:T(8,128)(2,1)} %bitcast.120, bf16[128,128,1]{1,0,2:T(8,128)(2,1)S(1)} %reshape.180, bf16[128,128,128]{1,2,0:T(8,128)(2,1)} %convert_bitcast_fusion), kind=kOutput, calls=%fused_computation.45 | convolution fusion | flops 1075855360 | bytes 8486912 | tf_op jit(solution)/shard_map/dot_general | solution.py:38
  136.6 1.7 slice_bitcast_fusion.3
  138.3 1.8 %slice_bitcast_fusion.2 = (bf16[32,128,128]{1,2,0:T(8,128)(2,1)S(1)}, bf16[32,128,128]{1,2,0:T(8,128)(2,1)S(1)}) fusion(bf16[2,32,128,128]{2,3,1,0:T(8,128)(2,1)} %collective-permute-done.5), kind=kLoop, calls=%fused_computation.52 | loop fusion | bytes 4194304 | tf_op jit(solution)/shard_map/squeeze | solution.py:63
  140.5 1.4 fusion.55
  142.1 1.4 fusion.45
  143.5 3.2 %fusion.84 = f32[128,128]{0,1:T(8,128)S(1)} fusion(f32[128,128]{0,1:T(8,128)S(1)} %fusion.55, bf16[32,128,128]{1,2,0:T(8,128)(2,1)} %collective-permute-done.1, bf16[32,128,128]{1,2,0:T(8,128)(2,1)} %collective-permute-done, bf16[128,64,128]{2,1,0:T(8,128)(2,1)S(1)} %get-tuple-element.5), kind=kOutput, calls=%fused_computation.47 | convolution fusion | flops 269516800 | bytes 4325376 | tf_op jit(solution)/shard_map/dot_general | solution.py:38
  146.8 3.1 %fusion.94 = f32[128,128]{0,1:T(8,128)S(1)} fusion(f32[128,128]{0,1:T(8,128)S(1)} %fusion.45, bf16[32,128,128]{1,2,0:T(8,128)(2,1)} %collective-permute-done.4, bf16[32,128,128]{1,2,0:T(8,128)(2,1)} %collective-permute-done.2, bf16[128,64,128]{2,1,0:T(8,128)(2,1)S(1)} %copy-done.4), kind=kOutput, calls=%fused_computation.49 | convolution fusion | flops 269516800 | bytes 4325376 | tf_op jit(solution)/shard_map/dot_general | solution.py:38
  150.2 24.8 %all_to_all.26 = f32[8,128,384]{2,1,0:T(8,128)S(1)} all-to-all(f32[8,128,384]{2,1,0:T(8,128)S(1)} %broadcast_multiply_fusion), channel_id=1, replica_groups=mesh['tau'=8,'blk'=64] {'tau'}, dimensions={0} | all-to-all | bytes 3145728 | tf_op jit(solution)/shard_map/all_to_all | solution.py:103
  (57 shorter events, 6.7 us)
Async XLA Ops:
  0.0 30.7 %copy-start = (bf16[1,8,2048]{2,1,0:T(8,128)(2,1)S(1)}, bf16[1,8,2048]{2,1,0:T(8,128)(2,1)}, u32[]{:S(2)}) copy-start(bf16[1,8,2048]{2,1,0:T(8,128)(2,1)} %param.6) | copy-start | bytes 98308
  33.4 33.3 %all-to-all-start.1 = ((bf16[64,2,2048]{2,1,0:T(2,128)(2,1)}), bf16[64,2,2048]{2,1,0:T(2,128)(2,1)S(1)}, u32[]{:S(2)}, u32[]{:S(2)}) async-start(bf16[64,2,2048]{2,1,0:T(2,128)(2,1)} %broadcast_select_fusion), calls=%async_computation.1 | async-start | bytes 1048576 | tf_op jit(solution)/shard_map/all_to_all | solution.py:90
  41.8 35.0 %collective-permute-start = (bf16[32,128,128]{1,2,0:T(8,128)(2,1)}, bf16[32,128,128]{1,2,0:T(8,128)(2,1)}, u32[]{:S(2)}, u32[]{:S(2)}) collective-permute-start(bf16[32,128,128]{1,2,0:T(8,128)(2,1)} %bitcast.123), channel_id=1, source_target_pairs={{0,1},{1,2},{2,3},{3,4},{4,5},{5,6},{6,7},{7,8},{8,9},{9,10},{10,1... | collective-permute-start | bytes 3145736 | tf_op jit(solution)/shard_map/ppermute | solution.py:14
  44.6 32.2 %collective-permute-start.2 = (bf16[32,128,128]{1,2,0:T(8,128)(2,1)}, bf16[32,128,128]{1,2,0:T(8,128)(2,1)}, u32[]{:S(2)}, u32[]{:S(2)}) collective-permute-start(bf16[32,128,128]{1,2,0:T(8,128)(2,1)} %bitcast.124), channel_id=1, source_target_pairs={{0,63},{1,0},{2,1},{3,2},{4,3},{5,4},{6,5},{7,6},{8,7},{9,8},{10,9... | collective-permute-start | bytes 3145736 | tf_op jit(solution)/shard_map/ppermute | solution.py:14
  51.4 47.9 %collective-permute-start.1 = (bf16[32,128,128]{1,2,0:T(8,128)(2,1)S(1)}, bf16[32,128,128]{1,2,0:T(8,128)(2,1)}, u32[]{:S(2)}, u32[]{:S(2)}) collective-permute-start(bf16[32,128,128]{1,2,0:T(8,128)(2,1)S(1)} %bitcast.121), channel_id=1, source_target_pairs={{0,1},{1,2},{2,3},{3,4},{4,5},{5,6},{6,7},{7,8},{8,9},{9,10},{10,1... | collective-permute-start | bytes 3145736 | tf_op jit(solution)/shard_map/ppermute | solution.py:14
  53.3 45.9 %collective-permute-start.4 = (bf16[32,128,128]{1,2,0:T(8,128)(2,1)S(1)}, bf16[32,128,128]{1,2,0:T(8,128)(2,1)}, u32[]{:S(2)}, u32[]{:S(2)}) collective-permute-start(bf16[32,128,128]{1,2,0:T(8,128)(2,1)S(1)} %bitcast.122), channel_id=1, source_target_pairs={{0,63},{1,0},{2,1},{3,2},{4,3},{5,4},{6,5},{7,6},{8,7},{9,8},{10,9... | collective-permute-start | bytes 3145736 | tf_op jit(solution)/shard_map/ppermute | solution.py:14
  60.0 6.7 %copy-start.6 = (s32[48]{0:T(128)S(1)}, s32[48]{0:T(128)}, u32[]{:S(2)}) copy-start(s32[48]{0:T(128)} %param.7) | copy-start | bytes 580
  79.8 56.7 %collective-permute-start.3 = (bf16[2,32,128,128]{2,3,1,0:T(8,128)(2,1)}, bf16[2,32,128,128]{2,3,1,0:T(8,128)(2,1)}, u32[]{:S(2)}, u32[]{:S(2)}) collective-permute-start(bf16[2,32,128,128]{2,3,1,0:T(8,128)(2,1)} %pad_maximum_fusion), channel_id=1, source_target_pairs={{0,64},{64,0},{128,192},{192,128},{256,320},{320,256},{384,448},{4... | collective-permute-start | bytes 6291464 | tf_op jit(solution)/shard_map/ppermute | solution.py:60
  99.2 7.2 %copy-start.2 = (bf16[128,128,128]{2,1,0:T(8,128)(2,1)S(1)}, bf16[128,128,128]{2,1,0:T(8,128)(2,1)}, u32[]{:S(2)}) copy-start(bf16[128,128,128]{2,1,0:T(8,128)(2,1)} %fusion.19) | copy-start | bytes 12582916
  102.5 35.8 %collective-permute-start.5 = (bf16[2,32,128,128]{2,3,1,0:T(8,128)(2,1)}, bf16[2,32,128,128]{2,3,1,0:T(8,128)(2,1)}, u32[]{:S(2)}, u32[]{:S(2)}) collective-permute-start(bf16[2,32,128,128]{2,3,1,0:T(8,128)(2,1)} %pad_maximum_fusion.1), channel_id=1, source_target_pairs={{0,64},{64,0},{128,192},{192,128},{256,320},{320,256},{384,448},{4... | collective-permute-start | bytes 6291464 | tf_op jit(solution)/shard_map/ppermute | solution.py:60
  115.8 5.4 %copy-start.1 = (bf16[128,128,128]{2,1,0:T(8,128)(2,1)S(1)}, bf16[128,128,128]{2,1,0:T(8,128)(2,1)}, u32[]{:S(2)}) copy-start(bf16[128,128,128]{2,1,0:T(8,128)(2,1)} %copy.63) | copy-start | bytes 12582916
  138.3 2.2 %copy-start.3 = (bf16[128,64,128]{2,1,0:T(8,128)(2,1)S(1)}, bf16[128,64,128]{2,1,0:T(8,128)(2,1)}, u32[]{:S(2)}) copy-start(bf16[128,64,128]{2,1,0:T(8,128)(2,1)} %get-tuple-element.6) | copy-start | bytes 6291460
  140.5 1.6 copy-start.5
  143.5 3.2 %copy-start.4 = (bf16[128,64,128]{2,1,0:T(8,128)(2,1)S(1)}, bf16[128,64,128]{2,1,0:T(8,128)(2,1)}, u32[]{:S(2)}) copy-start(bf16[128,64,128]{2,1,0:T(8,128)(2,1)} %get-tuple-element.7) | copy-start | bytes 6291460
  146.8 3.3 %copy-start.7 = (f32[8,1]{0,1:T(1,128)S(1)}, f32[8,1]{0,1:T(1,128)}, u32[]{:S(2)}) copy-start(f32[8,1]{0,1:T(1,128)} %param.9) | copy-start | bytes 100

commit v5 on v3

--- a/solution.py
+++ b/solution.py
@@ -79,7 +79,7 @@
         owner_match[:, :, None] * place_match[:, None, :] * block_slot[:, None, None], axis=0
     )
     asked = lax.all_to_all(outgoing, "blk", split_axis=0, concat_axis=0, tiled=True)
-    found_blocks = jnp.take(local_table, asked, axis=0)
+    found_blocks = jnp.take(local_table, asked, axis=0, mode="clip")
     replies = lax.all_to_all(found_blocks, "blk", split_axis=0, concat_axis=0, tiled=True)
     fetched = replies[block_owner, position]
     pieces = []
@@ -87,9 +87,7 @@
         occupied, virtual = green_pair(fetched[slot_index * per_slot : (slot_index + 1) * per_slot])
         image = image_of(occupied, virtual, source_t)
         if slot_index == HALF:
-            half = image.shape[1] // 2
-            own_part = pair_block(own_t[:half], image[:, :half]) + pair_block(own_t[half:], image[:, half:])
-            pieces.append(-2.0 * own_part)
+            pieces.append(-2.0 * pair_block(partners[slot_index], image))
         else:
             pieces.append(-2.0 * split_pair_block(partners[slot_index], image))
     chi_time = jnp.concatenate(pieces, axis=1)

time: 160 us -> 153 us (0.956)
  local copies, waits for them, and re-layouts: 32.3 us -> 21.9 us
  matrix products: 35.6 us -> 39.7 us
    unnamed x9 -> x8, local copies, waits for them, and re-layouts: 6.93 us -> 0.02 us
    dot_general x3 -> x2, matrix products: 19.8 us -> 13 us  [image_of(): lax.dot_general(halfway, occupied, (((1,), (1,)), ((), ())), preferred_el...]
    dot_general x6 -> x5, matrix products: 15.8 us -> 21.3 us  [pair_block(): return jnp.dot(flat_image, flat_partner, preferred_element_type=jnp.float32)]
    dot_general x0 -> x1, matrix products: none -> 5.37 us  [image_of(): lax.dot_general(source_t, virtual, (((2,), (1,)), ((), ())), preferred_el...]
    slice x1 -> x0, local copies, waits for them, and re-layouts: 4.54 us -> none  [local_body(): image[:, half:]]
  transfers between devices with their start and end apart: 9 -> 9, of which waited for: 0 -> 0; matrix products, arithmetic and copies ran while one was open for 40% -> 37% of each run, Pallas kernels for 0% -> 0%
where the time goes in v5:
time: 153 us
  blocking collectives  52.9 us (35%)
  matrix products  39.7 us (26%)
  starting transfers between devices  33.5 us (22%)
  local copies, waits for them, and re-layouts  21.9 us (14%)
  other arithmetic  4.09 us (3%)
    all_to_all x1, blocking collectives, local_body(): lax.all_to_all(outgoing, 'blk', split_axis=0, concat_axis=0, tiled=True)  27.8 us
    all_to_all x1, blocking collectives, local_body(): lax.all_to_all(weighted, 'tau', split_axis=0, concat_axis=0, tiled=True)  25.2 us
    dot_general x5, matrix products, pair_block(): return jnp.dot(flat_image, flat_partner, preferred_element_type=jnp.float32)  21.3 us
    ppermute x4, starting transfers between devices, from_behind(): lax.ppermute(value, axis, [(i, (i + by) % size) for i in range(size)])  17.2 us
    dot_general x2, matrix products, image_of(): lax.dot_general(halfway, occupied, (((1,), (1,)), ((), ())), preferred_el...  13 us
    ppermute x4, starting transfers between devices, partner_from(): other.append(lax.ppermute(got, 'tau', [(i, i ^ 1) for i in range(size)]))  11.6 us
    transpose x1, local copies, waits for them, and re-layouts, local_body(): source_t = jnp.transpose(source, (2, 0, 1))  6.75 us
    dot_general x1, matrix products, image_of(): lax.dot_general(source_t, virtual, (((2,), (1,)), ((), ())), preferred_el...  5.37 us
  transfers between devices with their start and end apart: 9, of which 0 were waited for; matrix products, arithmetic and copies ran while one was open for 37% of the time, Pallas kernels for 0%

profile of v5, /device:TPU:1, one launch (start us, length us, event | category | flops | bytes accessed | tf_op | source)
XLA Modules:
  0.0 152.6 jit_solution(1601621649940638055)
XLA Ops:
  0.0 0.7 fusion.99
  0.8 0.8 select_reduce_fusion
  1.7 0.8 multiply_reduce_fusion
  2.5 27.8 %all_to_all.19 = s32[64,1,2]{2,1,0:T(1,128)S(1)} all-to-all(s32[64,1,2]{2,1,0:T(1,128)S(1)} %copy.51), channel_id=1, replica_groups=mesh['tau'=8,'blk'=64] {'blk'}, dimensions={0} | all-to-all | bytes 1024 | tf_op jit(solution)/shard_map/all_to_all | solution.py:81
  31.7 0.9 gather_fusion
  32.7 1.1 reshape.123
  33.8 4.6 %all-to-all-start.1 = ((bf16[64,2,2048]{2,1,0:T(2,128)(2,1)}), bf16[64,2,2048]{2,1,0:T(2,128)(2,1)S(1)}, u32[]{:S(2)}, u32[]{:S(2)}) async-start(bf16[64,2,2048]{2,1,0:T(2,128)(2,1)} %reshape.123), calls=%async_computation.1 | async-start | bytes 1048576 | tf_op jit(solution)/shard_map/all_to_all | solution.py:83
  38.5 1.9 %constant_dynamic-slice_fusion.4 = (bf16[1,128,32,128]{3,2,1,0:T(8,128)(2,1)S(1)}, bf16[1,128,32,128]{3,2,1,0:T(8,128)(2,1)S(1)}) fusion(bf16[1,128,128,128]{3,2,1,0:T(8,128)(2,1)} %param.5, s32[]{:T(128)S(6)} %select_n.43, s32[]{:T(128)S(6)} %select_n.44), kind=kLoop, calls=%fused_computation.68 | loop fusion | bytes 4194312 | tf_op jit(solution)/shard_map/dynamic-slice.2
  40.4 1.7 %copy.55 = bf16[1,128,32,128]{1,3,2,0:T(8,128)(2,1)} copy(bf16[1,128,32,128]{3,2,1,0:T(8,128)(2,1)S(1)} %get-tuple-element.9) | data formatting | bytes 2097152 | tf_op jit(solution)/shard_map/dynamic-slice.2
  42.1 2.8 %collective-permute-start = (bf16[32,128,128]{1,2,0:T(8,128)(2,1)}, bf16[32,128,128]{1,2,0:T(8,128)(2,1)}, u32[]{:S(2)}, u32[]{:S(2)}) collective-permute-start(bf16[32,128,128]{1,2,0:T(8,128)(2,1)} %bitcast.103), channel_id=1, source_target_pairs={{0,1},{1,2},{2,3},{3,4},{4,5},{5,6},{6,7},{7,8},{8,9},{9,10},{10,1... | collective-permute-start | bytes 3145736 | tf_op jit(solution)/shard_map/ppermute | solution.py:14
  44.9 5.8 %collective-permute-start.4 = (bf16[32,128,128]{1,2,0:T(8,128)(2,1)}, bf16[32,128,128]{1,2,0:T(8,128)(2,1)}, u32[]{:S(2)}, u32[]{:S(2)}) collective-permute-start(bf16[32,128,128]{1,2,0:T(8,128)(2,1)} %bitcast.104), channel_id=1, source_target_pairs={{0,63},{1,0},{2,1},{3,2},{4,3},{5,4},{6,5},{7,6},{8,7},{9,8},{10,9... | collective-permute-start | bytes 3145736 | tf_op jit(solution)/shard_map/ppermute | solution.py:14
  50.7 1.0 copy.56
  51.7 1.9 %collective-permute-start.1 = (bf16[32,128,128]{1,2,0:T(8,128)(2,1)S(1)}, bf16[32,128,128]{1,2,0:T(8,128)(2,1)}, u32[]{:S(2)}, u32[]{:S(2)}) collective-permute-start(bf16[32,128,128]{1,2,0:T(8,128)(2,1)S(1)} %bitcast.105), channel_id=1, source_target_pairs={{0,1},{1,2},{2,3},{3,4},{4,5},{5,6},{6,7},{7,8},{8,9},{9,10},{10,1... | collective-permute-start | bytes 3145736 | tf_op jit(solution)/shard_map/ppermute | solution.py:14
  53.6 6.7 %collective-permute-start.5 = (bf16[32,128,128]{1,2,0:T(8,128)(2,1)S(1)}, bf16[32,128,128]{1,2,0:T(8,128)(2,1)}, u32[]{:S(2)}, u32[]{:S(2)}) collective-permute-start(bf16[32,128,128]{1,2,0:T(8,128)(2,1)S(1)} %bitcast.106), channel_id=1, source_target_pairs={{0,63},{1,0},{2,1},{3,2},{4,3},{5,4},{6,5},{7,6},{8,7},{9,8},{10,9... | collective-permute-start | bytes 3145736 | tf_op jit(solution)/shard_map/ppermute | solution.py:14
  60.3 6.8 %copy.53 = bf16[128,128,128]{2,1,0:T(8,128)(2,1)} copy(bf16[128,128,128]{0,2,1:T(8,128)(2,1)} %bitcast.101) | data formatting | bytes 8388608 | tf_op jit(solution)/shard_map/transpose | solution.py:65
  67.1 1.2 gather_fusion.1
  69.8 6.5 %fusion.19 = bf16[128,128,128]{2,1,0:T(8,128)(2,1)} fusion(bf16[128,128,1]{1,0,2:T(8,128)(2,1)S(1)} %reshape.144, bf16[128,128,1]{1,0,2:T(8,128)(2,1)S(1)} %reshape.143, bf16[128,128,128]{2,1,0:T(8,128)(2,1)} %copy.53), kind=kOutput, calls=%fused_computation.16 | convolution fusion | flops 1077936128 | bytes 8454144 | tf_op jit(solution)/shard_map/dot_general | solution.py:28
  76.4 6.5 %fusion.22 = bf16[128,128,128]{2,1,0:T(8,128)(2,1)} fusion(bf16[128,128,1]{1,0,2:T(8,128)(2,1)S(1)} %reshape.151, bf16[128,128,1]{1,0,2:T(8,128)(2,1)S(1)} %reshape.150, bf16[128,128,128]{2,1,0:T(8,128)(2,1)} %copy.53), kind=kOutput, calls=%fused_computation.17 | convolution fusion | flops 1077936128 | bytes 8454144 | tf_op jit(solution)/shard_map/dot_general | solution.py:28
  83.3 5.4 %convert_bitcast_fusion = bf16[128,128,128]{1,2,0:T(8,128)(2,1)} fusion(bf16[128,128,1]{1,0,2:T(8,128)(2,1)S(1)} %reshape.147, bf16[128,128,128]{2,1,0:T(8,128)(2,1)} %copy.53), kind=kOutput, calls=%fused_computation.12 | convolution fusion | flops 538968064 | bytes 8421376 | tf_op jit(solution)/shard_map/dot_general | solution.py:25
  88.6 12.2 %fusion.72 = f32[128,128]{0,1:T(8,128)S(1)} fusion(bf16[128,128,128]{2,0,1:T(8,128)(2,1)} %bitcast.102, bf16[128,128,1]{1,0,2:T(8,128)(2,1)S(1)} %reshape.148, bf16[128,128,128]{1,2,0:T(8,128)(2,1)} %convert_bitcast_fusion), kind=kOutput, calls=%fused_computation.43 | convolution fusion | flops 1075855360 | bytes 8486912 | tf_op jit(solution)/shard_map/dot_general | solution.py:38
  100.8 5.1 %collective-permute-start.2 = (bf16[32,128,128]{1,2,0:T(8,128)(2,1)}, bf16[32,128,128]{1,2,0:T(8,128)(2,1)S(1)}, u32[]{:S(2)}, u32[]{:S(2)}) collective-permute-start(bf16[32,128,128]{1,2,0:T(8,128)(2,1)} %collective-permute-done), channel_id=1, source_target_pairs={{0,64},{64,0},{128,192},{192,128},{256,320},{320,256},{384,448},{4... | collective-permute-start | bytes 3145736 | tf_op jit(solution)/shard_map/ppermute | solution.py:59
  106.0 1.9 %collective-permute-start.3 = (bf16[32,128,128]{1,2,0:T(8,128)(2,1)}, bf16[32,128,128]{1,2,0:T(8,128)(2,1)S(1)}, u32[]{:S(2)}, u32[]{:S(2)}) collective-permute-start(bf16[32,128,128]{1,2,0:T(8,128)(2,1)} %collective-permute-done.1), channel_id=1, source_target_pairs={{0,64},{64,0},{128,192},{192,128},{256,320},{320,256},{384,448},{4... | collective-permute-start | bytes 3145736 | tf_op jit(solution)/shard_map/ppermute | solution.py:59
  107.9 3.4 %constant_dynamic-slice_fusion.2 = (bf16[128,64,128]{2,1,0:T(8,128)(2,1)S(1)}, bf16[128,64,128]{2,1,0:T(8,128)(2,1)S(1)}) fusion(bf16[128,128,128]{2,1,0:T(8,128)(2,1)} %fusion.19, s32[]{:T(128)S(6)} %select_n.45, s32[]{:T(128)S(6)} %select_n.43), kind=kLoop, calls=%fused_computation.66 | loop fusion | bytes 8388616 | tf_op jit(solution)/shard_map/dynamic_slice | solution.py:45
  111.3 2.4 %collective-permute-start.6 = (bf16[32,128,128]{1,2,0:T(8,128)(2,1)}, bf16[32,128,128]{1,2,0:T(8,128)(2,1)S(1)}, u32[]{:S(2)}, u32[]{:S(2)}) collective-permute-start(bf16[32,128,128]{1,2,0:T(8,128)(2,1)} %collective-permute-done.4), channel_id=1, source_target_pairs={{0,64},{64,0},{128,192},{192,128},{256,320},{320,256},{384,448},{4... | collective-permute-start | bytes 3145736 | tf_op jit(solution)/shard_map/ppermute | solution.py:59
  113.7 2.2 %collective-permute-start.7 = (bf16[32,128,128]{1,2,0:T(8,128)(2,1)}, bf16[32,128,128]{1,2,0:T(8,128)(2,1)S(1)}, u32[]{:S(2)}, u32[]{:S(2)}) collective-permute-start(bf16[32,128,128]{1,2,0:T(8,128)(2,1)} %collective-permute-done.5), channel_id=1, source_target_pairs={{0,64},{64,0},{128,192},{192,128},{256,320},{320,256},{384,448},{4... | collective-permute-start | bytes 3145736 | tf_op jit(solution)/shard_map/ppermute | solution.py:59
  115.9 1.2 constant_dynamic-slice_fusion
  117.1 3.0 %fusion.60 = f32[128,128]{0,1:T(8,128)S(1)} fusion(bf16[32,128,128]{1,2,0:T(8,128)(2,1)} %collective-permute-done.1, bf16[32,128,128]{1,2,0:T(8,128)(2,1)} %collective-permute-done, bf16[128,64,128]{2,1,0:T(8,128)(2,1)S(1)} %get-tuple-element.6), kind=kOutput, calls=%fused_computation.41 | convolution fusion | flops 269484032 | bytes 4259840 | tf_op jit(solution)/shard_map/dot_general | solution.py:38
  120.1 3.0 %fusion.50 = f32[128,128]{0,1:T(8,128)S(1)} fusion(bf16[32,128,128]{1,2,0:T(8,128)(2,1)} %collective-permute-done.5, bf16[32,128,128]{1,2,0:T(8,128)(2,1)} %collective-permute-done.4, bf16[128,64,128]{2,1,0:T(8,128)(2,1)S(1)} %get-tuple-element.8), kind=kOutput, calls=%fused_computation.39 | convolution fusion | flops 269484032 | bytes 4259840 | tf_op jit(solution)/shard_map/dot_general | solution.py:38
  123.2 1.6 %fusion.84 = f32[128,128]{0,1:T(8,128)S(1)} fusion(f32[128,128]{0,1:T(8,128)S(1)} %fusion.60, bf16[32,128,128]{1,2,0:T(8,128)(2,1)S(1)} %collective-permute-done.3, bf16[32,128,128]{1,2,0:T(8,128)(2,1)S(1)} %collective-permute-done.2, bf16[128,64,128]{2,1,0:T(8,128)(2,1)S(1)} %get-tuple-element.5), kind=kOutput, calls=%fused_computation.45 | convolution fusion | flops 269516800 | bytes 4325376 | tf_op jit(solution)/shard_map/dot_general | solution.py:38
  124.8 1.5 %fusion.94 = f32[128,128]{0,1:T(8,128)S(1)} fusion(f32[128,128]{0,1:T(8,128)S(1)} %fusion.50, bf16[32,128,128]{1,2,0:T(8,128)(2,1)S(1)} %collective-permute-done.7, bf16[32,128,128]{1,2,0:T(8,128)(2,1)S(1)} %collective-permute-done.6, bf16[128,64,128]{2,1,0:T(8,128)(2,1)S(1)} %get-tuple-element.7), kind=kOutput, calls=%fused_computation.47 | convolution fusion | flops 269516800 | bytes 4325376 | tf_op jit(solution)/shard_map/dot_general | solution.py:38
  126.6 25.2 %all_to_all.20 = f32[8,128,384]{2,1,0:T(8,128)S(1)} all-to-all(f32[8,128,384]{2,1,0:T(8,128)S(1)} %broadcast_multiply_fusion), channel_id=1, replica_groups=mesh['tau'=8,'blk'=64] {'tau'}, dimensions={0} | all-to-all | bytes 3145728 | tf_op jit(solution)/shard_map/all_to_all | solution.py:96
  151.8 0.8 reduce_sum.29
  (45 shorter events, 3.7 us)
Async XLA Ops:
  0.0 31.7 %copy-start = (bf16[1,8,2048]{2,1,0:T(8,128)(2,1)S(1)}, bf16[1,8,2048]{2,1,0:T(8,128)(2,1)}, u32[]{:S(2)}) copy-start(bf16[1,8,2048]{2,1,0:T(8,128)(2,1)} %param.6) | copy-start | bytes 98308
  33.8 33.3 %all-to-all-start.1 = ((bf16[64,2,2048]{2,1,0:T(2,128)(2,1)}), bf16[64,2,2048]{2,1,0:T(2,128)(2,1)S(1)}, u32[]{:S(2)}, u32[]{:S(2)}) async-start(bf16[64,2,2048]{2,1,0:T(2,128)(2,1)} %reshape.123), calls=%async_computation.1 | async-start | bytes 1048576 | tf_op jit(solution)/shard_map/all_to_all | solution.py:83
  42.1 58.7 %collective-permute-start = (bf16[32,128,128]{1,2,0:T(8,128)(2,1)}, bf16[32,128,128]{1,2,0:T(8,128)(2,1)}, u32[]{:S(2)}, u32[]{:S(2)}) collective-permute-start(bf16[32,128,128]{1,2,0:T(8,128)(2,1)} %bitcast.103), channel_id=1, source_target_pairs={{0,1},{1,2},{2,3},{3,4},{4,5},{5,6},{6,7},{7,8},{8,9},{9,10},{10,1... | collective-permute-start | bytes 3145736 | tf_op jit(solution)/shard_map/ppermute | solution.py:14
  44.9 66.4 %collective-permute-start.4 = (bf16[32,128,128]{1,2,0:T(8,128)(2,1)}, bf16[32,128,128]{1,2,0:T(8,128)(2,1)}, u32[]{:S(2)}, u32[]{:S(2)}) collective-permute-start(bf16[32,128,128]{1,2,0:T(8,128)(2,1)} %bitcast.104), channel_id=1, source_target_pairs={{0,63},{1,0},{2,1},{3,2},{4,3},{5,4},{6,5},{7,6},{8,7},{9,8},{10,9... | collective-permute-start | bytes 3145736 | tf_op jit(solution)/shard_map/ppermute | solution.py:14
  51.7 54.3 %collective-permute-start.1 = (bf16[32,128,128]{1,2,0:T(8,128)(2,1)S(1)}, bf16[32,128,128]{1,2,0:T(8,128)(2,1)}, u32[]{:S(2)}, u32[]{:S(2)}) collective-permute-start(bf16[32,128,128]{1,2,0:T(8,128)(2,1)S(1)} %bitcast.105), channel_id=1, source_target_pairs={{0,1},{1,2},{2,3},{3,4},{4,5},{5,6},{6,7},{7,8},{8,9},{9,10},{10,1... | collective-permute-start | bytes 3145736 | tf_op jit(solution)/shard_map/ppermute | solution.py:14
  53.6 60.1 %collective-permute-start.5 = (bf16[32,128,128]{1,2,0:T(8,128)(2,1)S(1)}, bf16[32,128,128]{1,2,0:T(8,128)(2,1)}, u32[]{:S(2)}, u32[]{:S(2)}) collective-permute-start(bf16[32,128,128]{1,2,0:T(8,128)(2,1)S(1)} %bitcast.106), channel_id=1, source_target_pairs={{0,63},{1,0},{2,1},{3,2},{4,3},{5,4},{6,5},{7,6},{8,7},{9,8},{10,9... | collective-permute-start | bytes 3145736 | tf_op jit(solution)/shard_map/ppermute | solution.py:14
  60.3 6.8 %copy-start.2 = (s32[48]{0:T(128)S(1)}, s32[48]{0:T(128)}, u32[]{:S(2)}) copy-start(s32[48]{0:T(128)} %param.7) | copy-start | bytes 580
  100.8 22.3 %collective-permute-start.2 = (bf16[32,128,128]{1,2,0:T(8,128)(2,1)}, bf16[32,128,128]{1,2,0:T(8,128)(2,1)S(1)}, u32[]{:S(2)}, u32[]{:S(2)}) collective-permute-start(bf16[32,128,128]{1,2,0:T(8,128)(2,1)} %collective-permute-done), channel_id=1, source_target_pairs={{0,64},{64,0},{128,192},{192,128},{256,320},{320,256},{384,448},{4... | collective-permute-start | bytes 3145736 | tf_op jit(solution)/shard_map/ppermute | solution.py:59
  106.0 17.2 %collective-permute-start.3 = (bf16[32,128,128]{1,2,0:T(8,128)(2,1)}, bf16[32,128,128]{1,2,0:T(8,128)(2,1)S(1)}, u32[]{:S(2)}, u32[]{:S(2)}) collective-permute-start(bf16[32,128,128]{1,2,0:T(8,128)(2,1)} %collective-permute-done.1), channel_id=1, source_target_pairs={{0,64},{64,0},{128,192},{192,128},{256,320},{320,256},{384,448},{4... | collective-permute-start | bytes 3145736 | tf_op jit(solution)/shard_map/ppermute | solution.py:59
  107.9 8.0 %copy-start.1 = (bf16[128,128,128]{2,1,0:T(8,128)(2,1)S(1)}, bf16[128,128,128]{2,1,0:T(8,128)(2,1)}, u32[]{:S(2)}) copy-start(bf16[128,128,128]{2,1,0:T(8,128)(2,1)} %fusion.22) | copy-start | bytes 12582916
  111.3 13.4 %collective-permute-start.6 = (bf16[32,128,128]{1,2,0:T(8,128)(2,1)}, bf16[32,128,128]{1,2,0:T(8,128)(2,1)S(1)}, u32[]{:S(2)}, u32[]{:S(2)}) collective-permute-start(bf16[32,128,128]{1,2,0:T(8,128)(2,1)} %collective-permute-done.4), channel_id=1, source_target_pairs={{0,64},{64,0},{128,192},{192,128},{256,320},{320,256},{384,448},{4... | collective-permute-start | bytes 3145736 | tf_op jit(solution)/shard_map/ppermute | solution.py:59
  113.7 11.0 %collective-permute-start.7 = (bf16[32,128,128]{1,2,0:T(8,128)(2,1)}, bf16[32,128,128]{1,2,0:T(8,128)(2,1)S(1)}, u32[]{:S(2)}, u32[]{:S(2)}) collective-permute-start(bf16[32,128,128]{1,2,0:T(8,128)(2,1)} %collective-permute-done.5), channel_id=1, source_target_pairs={{0,64},{64,0},{128,192},{192,128},{256,320},{320,256},{384,448},{4... | collective-permute-start | bytes 3145736 | tf_op jit(solution)/shard_map/ppermute | solution.py:59
  124.8 1.7 %copy-start.3 = (f32[8,1]{0,1:T(1,128)S(1)}, f32[8,1]{0,1:T(1,128)}, u32[]{:S(2)}) copy-start(f32[8,1]{0,1:T(1,128)} %param.9) | copy-start | bytes 100
